TPU v7x, 256 devices: a whole 4x4x8 slice. The times are simulated.
256 devices in a mesh: gx: 32 (over z_hi, y, core), gy: 8 (over z_lo, x).
Axes of the slice: x: 4, y: 4, z: 8 (z_hi: 4, z_lo: 2; z = z_hi * 2 + z_lo), core: 2. Of those that a mesh axis runs over, the one named last changes fastest.
Arguments:
- state: float32 [5, 256, 64, 128], P(None, 'gx', 'gy'), may hold values from -6 to 6
- terrain: int32 [256, 64], P('gx', 'gy'), may hold values from 0 to 31
- site_cells: int32 [65536], P(('gx', 'gy')), may hold values from 0 to 8191
- site_values: float32 [5, 65536], P(None, ('gx', 'gy')), may hold values from -6 to 6
- w_in: float32 [64, 4], replicated, may hold values from -3 to 3
- b_in: float32 [64], replicated, may hold values from -3 to 3
- w_out: float32 [64], replicated, may hold values from -1.5 to 1.5
Outputs:
- state_grad: float32 [5, 256, 64, 128], P(None, 'gx', 'gy')
- closure_grad: float32 [64, 6], replicated
Inputs may be any that keep to these rules, and one draw needn't show every extreme that they name: `site_cells`: site s lies on the device that holds entry s; its id names a cell of that device's block as (i * 8 + j) * 128 + k for local position (i, j, k).
All inputs are finite; a program needn't handle non-finite values.
Results may differ from a plain program's by a relative error of at most 0.0003.
Values sent between devices are 32-bit elements; how exact they have to be, the bound alone decides.
No kernel may reach another device: no remote copies, remote signals or barrier semaphores. Data moves between devices by JAX's collectives and lax.ppermute only.
A program may use at most 128 MiB of HBM per device.

v0:
```python
import jax
import jax.numpy as jnp
from jax import lax
from jax.sharding import PartitionSpec as P

STEPS = 4


PRECISE = lax.Precision.HIGHEST


def padded_2(cells, sides, width):
    for axis, dim in sides:
        count = lax.axis_size(axis)
        ends = count - 1
        head = lax.slice_in_dim(cells, 0, width, axis=dim)
        tail = lax.slice_in_dim(cells, cells.shape[dim] - width, cells.shape[dim], axis=dim)
        cells = jnp.concatenate(
            [
                lax.ppermute(tail, axis, [(i, (i + 1) % count) for i in range(ends)]),
                cells,
                lax.ppermute(head, axis, [((i + 1) % count, i) for i in range(ends)]),
            ],
            axis=dim,
        )
    return cells


def faces_padded(cells, width):
    parts = []
    for axis, dim in (("gx", 1), ("gy", 2)):
        count = lax.axis_size(axis)
        ends = count - 1
        head = lax.slice_in_dim(cells, 0, width, axis=dim)
        tail = lax.slice_in_dim(cells, cells.shape[dim] - width, cells.shape[dim], axis=dim)
        parts.append(lax.ppermute(tail, axis, [(i, (i + 1) % count) for i in range(ends)]))
        parts.append(lax.ppermute(head, axis, [((i + 1) % count, i) for i in range(ends)]))
    low_x, high_x, low_y, high_y = parts
    middle = jnp.concatenate([low_y, cells, high_y], axis=2)
    shape = list(low_x.shape)
    shape[2] = width
    blank = jnp.zeros(shape, cells.dtype)
    low_x = jnp.concatenate([blank, low_x, blank], axis=2)
    high_x = jnp.concatenate([blank, high_x, blank], axis=2)
    return jnp.concatenate([low_x, middle, high_x], axis=1)


def vertical_diff(values):
    blank = jnp.zeros_like(values[..., :1])
    upper = jnp.concatenate([values[..., 1:], blank], axis=-1)
    lower = jnp.concatenate([blank, values[..., :-1]], axis=-1)
    return 0.5 * (upper - lower)


def closure_inputs(fields, terrain):
    levels = jnp.arange(fields.shape[-1], dtype=jnp.int32)
    height = 2.0 * (levels - terrain[..., None]).astype(jnp.float32) / fields.shape[-1]
    return jnp.stack(
        [vertical_diff(fields[0]), vertical_diff(fields[1]), vertical_diff(fields[2]), height]
    )


def spread(weights, ndim):
    return weights.reshape(weights.shape + (1,) * ndim)


def hidden_units(inputs, w_in, b_in):
    ndim = inputs.ndim - 1
    before = spread(w_in[:, 0], ndim) * inputs[0]
    for feature in range(1, inputs.shape[0]):
        before = before + spread(w_in[:, feature], ndim) * inputs[feature]
    return jnp.tanh(before + spread(b_in, ndim))


def logit_of(hidden, w_out):
    return jnp.sum(spread(w_out, hidden.ndim - 1) * hidden, axis=0)


def viscosity(hidden, w_out):
    return 0.16 * jax.nn.sigmoid(logit_of(hidden, w_out))


def interior(values):
    return values[..., 1:-1, 1:-1, :]


def beside(values):
    return [
        values[..., 2:, 1:-1, :],
        values[..., :-2, 1:-1, :],
        values[..., 1:-1, 2:, :],
        values[..., 1:-1, :-2, :],
    ]


def above_below(values):
    blank = jnp.zeros_like(values[..., :1])
    return [
        jnp.concatenate([values[..., 1:], blank], axis=-1),
        jnp.concatenate([blank, values[..., :-1]], axis=-1),
    ]


def fluid_cells(terrain, levels_count):
    levels = jnp.arange(levels_count, dtype=jnp.int32)
    return (levels >= terrain[..., None]).astype(jnp.float32)


def advance(fields, viscous, fluid):
    centre = interior(fields)
    visc_mid = interior(viscous)
    fluid_mid = interior(fluid)
    near_sets = list(zip(beside(fields), beside(viscous), beside(fluid)))
    near_sets = near_sets + list(
        zip(above_below(centre), above_below(visc_mid), above_below(fluid_mid))
    )
    summed = centre
    for field_near, visc_near, fluid_near in near_sets:
        conductance = fluid_mid * fluid_near * 0.5 * (visc_mid + visc_near)
        summed = summed + conductance * (field_near - centre)
    return summed


def crop(values, count, first):
    if count == 0:
        return values
    for dim in (first, first + 1):
        values = lax.slice_in_dim(values, count, values.shape[dim] - count, axis=dim)
    return values


def adjoint_step(padded, viscous, fluid, terrain, backward, w_in, b_in, w_out, core):
    centre = interior(padded)
    visc_mid = interior(viscous)
    fluid_mid = interior(fluid)
    back_mid = interior(backward)
    near_sets = list(zip(beside(padded), beside(viscous), beside(fluid), beside(backward)))
    near_sets = near_sets + list(
        zip(
            above_below(centre),
            above_below(visc_mid),
            above_below(fluid_mid),
            above_below(back_mid),
        )
    )
    result = back_mid
    visc_grad = jnp.zeros(visc_mid.shape, jnp.float32)
    for field_near, visc_near, fluid_near, back_near in near_sets:
        open_face = fluid_mid * fluid_near
        conductance = open_face * 0.5 * (visc_mid + visc_near)
        result = result + conductance * (back_near - back_mid)
        visc_grad = visc_grad + open_face * 0.5 * jnp.sum(
            (field_near - centre) * (back_mid - back_near), axis=0
        )
    inputs = closure_inputs(centre, terrain[1:-1, 1:-1])
    hidden = hidden_units(inputs, w_in, b_in)
    squash = jax.nn.sigmoid(logit_of(hidden, w_out))
    logit_grad = visc_grad * 0.16 * squash * (1.0 - squash)
    before_grad = spread(w_out, 3) * logit_grad * (1.0 - hidden * hidden)
    logit_core = crop(logit_grad, core, 0)
    hidden_core = crop(hidden, core, 1)
    before_core = crop(before_grad, core, 1)
    inputs_core = crop(inputs, core, 1)
    cells = (1, 2, 3)
    out_grad = jnp.sum(logit_core * hidden_core, axis=cells)
    in_grad = jnp.stack(
        [jnp.sum(before_core * inputs_core[feature], axis=cells) for feature in range(inputs.shape[0])],
        axis=1,
    )
    bias_grad = jnp.sum(before_core, axis=cells)
    input_grad = jnp.stack(
        [jnp.sum(spread(w_in[:, feature], 3) * before_grad, axis=0) for feature in range(3)]
    )
    result = result.at[:3].add(-vertical_diff(input_grad))
    partial_grad = jnp.concatenate([in_grad, bias_grad[:, None], out_grad[:, None]], axis=1)
    return (result, partial_grad)


def seed_from(final, site_cells, site_values):
    fields_count, width_x, width_y, levels_count = final.shape
    columns = width_x * width_y
    flat = final.reshape(fields_count, columns, levels_count)
    column_pick = (
        (site_cells // levels_count)[:, None] == jnp.arange(columns, dtype=jnp.int32)[None, :]
    ).astype(jnp.float32)
    level_pick = (
        (site_cells % levels_count)[:, None] == jnp.arange(levels_count, dtype=jnp.int32)[None, :]
    ).astype(jnp.float32)
    rows = jnp.einsum("sc,fck->sfk", column_pick, flat, precision=PRECISE)
    at_sites = jnp.sum(rows * level_pick[:, None, :], axis=-1)
    misfit = at_sites - site_values.T
    spread_rows = misfit[:, :, None] * level_pick[:, None, :]
    seed = jnp.einsum("sc,sfk->fck", column_pick, spread_rows, precision=PRECISE)
    return seed.reshape(final.shape)


def add_partial(grad_sum, partial_grad):
    return grad_sum + partial_grad


def butterfly_sum(values, axis):
    count = lax.axis_size(axis)
    if count & (count - 1):
        return lax.psum(values, axis)
    step = 1
    while step < count:
        values = values + lax.ppermute(values, axis, [(i, i ^ step) for i in range(count)])
        step *= 2
    return values


HALO = STEPS
BACK_HALO = 2


def body(state, terrain, site_cells, site_values, w_in, b_in, w_out):
    fields_count, width_x, width_y, levels_count = state.shape
    top_code = (levels_count - terrain).astype(jnp.float32)
    code_plane = jnp.broadcast_to(top_code[None, :, :, None], (1, width_x, width_y, levels_count))
    packed = padded_2(jnp.concatenate([state, code_plane], axis=0), (("gx", 1), ("gy", 2)), HALO)
    fields = packed[:fields_count]
    terrain_padded = levels_count - packed[fields_count, :, :, 0].astype(jnp.int32)
    fluid_padded = fluid_cells(terrain_padded, levels_count)
    grad_sum = jnp.zeros((w_in.shape[0], w_in.shape[1] + 2), jnp.float32)
    saved = []
    for step_index in range(STEPS):
        trim = step_index
        terrain_here = crop(terrain_padded, trim, 0)
        fluid_here = crop(fluid_padded, trim, 0)
        viscous = viscosity(hidden_units(closure_inputs(fields, terrain_here), w_in, b_in), w_out)
        saved.append((fields, viscous, fluid_here, terrain_here))
        fields = advance(fields, viscous, fluid_here)
    fields = crop(fields, HALO - STEPS, 1)
    backward = seed_from(fields, site_cells, site_values)
    reach = 0
    for step_index in range(STEPS - 1, -1, -1):
        if reach == 0:
            reach = min(BACK_HALO, step_index + 1, HALO - step_index)
            if reach == 1:
                backward = faces_padded(backward, reach)
            else:
                backward = padded_2(backward, (("gx", 1), ("gy", 2)), reach)
        padded, viscous, fluid_here, terrain_here = saved[step_index]
        trim = HALO - step_index - reach
        backward, partial_grad = adjoint_step(
            crop(padded, trim, 1),
            crop(viscous, trim, 0),
            crop(fluid_here, trim, 0),
            crop(terrain_here, trim, 0),
            backward,
            w_in,
            b_in,
            w_out,
            reach - 1,
        )
        reach -= 1
        grad_sum = add_partial(grad_sum, partial_grad)
    closure_sum = butterfly_sum(butterfly_sum(grad_sum, "gy"), "gx")
    site_total = site_cells.shape[0] * lax.axis_size("gx") * lax.axis_size("gy")
    return (backward, closure_sum * site_total ** (-0.5))


def solution(mesh):
    return jax.shard_map(
        body,
        mesh=mesh,
        in_specs=(
            P(None, "gx", "gy", None),
            P("gx", "gy"),
            P(("gx", "gy")),
            P(None, ("gx", "gy")),
            P(),
            P(),
            P(),
        ),
        out_specs=(P(None, "gx", "gy", None), P()),
        check_vma=False,
    )
```

profile of v0, /device:TPU:32, one launch (start us, length us, event | category | flops | bytes accessed | tf_op | source)
XLA Modules:
  0.0 182.8 jit_solution(1267951684505458334)
XLA Ops:
  0.6 0.7 subtract_convert_fusion
  1.4 0.9 fusion.132
  2.4 1.3 collective-permute-start.1
  3.7 3.0 %collective-permute-start = (f32[6,4,8,128]{3,2,1,0:T(8,128)S(1)}, f32[6,4,8,128]{3,2,1,0:T(8,128)S(1)}, u32[]{:S(2)}, u32[]{:S(2)}) collective-permute-start(f32[6,4,8,128]{3,2,1,0:T(8,128)S(1)} %get-tuple-element.201), channel_id=1, source_target_pairs={{0,8},{8,16},{16,24},{24,32},{32,40},{40,48},{48,56},{56,64},{64,7... | collective-permute-start | bytes 294920 | tf_op jit(solution)/shard_map/ppermute | solution.py:20
  6.7 0.8 slice_bitcast_fusion.26
  7.6 1.8 fusion.199
  9.3 0.7 and_select_fusion.1
  10.1 0.7 subtract_multiply_fusion.21
  10.9 0.7 subtract_multiply_fusion.22
  11.5 0.7 subtract_multiply_fusion.23
  12.4 4.2 %collective-permute-start.3 = (f32[6,16,4,128]{3,1,2,0:T(8,128)S(1)}, f32[6,16,4,128]{3,1,2,0:T(8,128)S(1)}, u32[]{:S(2)}, u32[]{:S(2)}) collective-permute-start(f32[6,16,4,128]{3,1,2,0:T(8,128)S(1)} %copy.262), channel_id=1, source_target_pairs={{1,0},{2,1},{3,2},{4,3},{5,4},{6,5},{7,6},{9,8},{10,9},{11,10},{12... | collective-permute-start | bytes 589832 | tf_op jit(solution)/shard_map/ppermute | solution.py:22
  16.6 1.9 %collective-permute-start.2 = (f32[6,16,4,128]{3,1,2,0:T(8,128)S(1)}, f32[6,16,4,128]{3,1,2,0:T(8,128)S(1)}, u32[]{:S(2)}, u32[]{:S(2)}) collective-permute-start(f32[6,16,4,128]{3,1,2,0:T(8,128)S(1)} %copy.261), channel_id=1, source_target_pairs={{0,1},{1,2},{2,3},{3,4},{4,5},{5,6},{6,7},{8,9},{9,10},{10,11},{11... | collective-permute-start | bytes 589832 | tf_op jit(solution)/shard_map/ppermute | solution.py:20
  18.6 3.3 %collective-permute-done.3 = f32[6,16,4,128]{3,1,2,0:T(8,128)S(1)} collective-permute-done((f32[6,16,4,128]{3,1,2,0:T(8,128)S(1)}, f32[6,16,4,128]{3,1,2,0:T(8,128)S(1)}, u32[]{:S(2)}, u32[]{:S(2)}) %collective-permute-start.3) | collective-permute-done | bytes 196640 | tf_op jit(solution)/shard_map/ppermute | solution.py:22
  21.9 6.4 %collective-permute-done.2 = f32[6,16,4,128]{3,1,2,0:T(8,128)S(1)} collective-permute-done((f32[6,16,4,128]{3,1,2,0:T(8,128)S(1)}, f32[6,16,4,128]{3,1,2,0:T(8,128)S(1)}, u32[]{:S(2)}, u32[]{:S(2)}) %collective-permute-start.2) | collective-permute-done | bytes 196640 | tf_op jit(solution)/shard_map/ppermute | solution.py:20
  30.0 3.7 %multiply_reduce_fusion = f32[16,16,128]{2,1,0:T(8,128)S(1)} fusion(f32[64]{0:T(128)S(1)} %copy-done.55, f32[16,16,128]{2,1,0:T(8,128)S(1)} %get-tuple-element.316, f32[64]{0:T(128)S(1)} %get-tuple-element.310, f32[16,16,128]{2,1,0:T(8,128)S(1)} %get-tuple-element.317, f32[64]{0:T(128)S(1)} %get-tuple-element.311, ...), kind=kLoop, calls=%fused_computation | loop fusion | flops 20938752 | bytes 656896 | tf_op jit(solution)/shard_map/reduce_sum | solution.py:76
  35.9 3.6 %multiply_reduce_fusion.1 = f32[14,14,128]{2,1,0:T(8,128)S(1)} fusion(f32[64]{0:T(128)S(1)} %copy-done.55, f32[14,14,128]{2,1,0:T(8,128)S(1)} %convert_multiply_fusion.1, f32[64]{0:T(128)S(1)} %get-tuple-element.310, f32[14,14,128]{2,1,0:T(8,128)S(1)} %subtract_multiply_fusion.7, f32[64]{0:T(128)S(1)} %get-tuple-element.311, ...), kind=kLoop, calls=%fused_computation.1 | loop fusion | flops 16031232 | bytes 503296 | tf_op jit(solution)/shard_map/reduce_sum | solution.py:76
  41.4 2.3 %multiply_reduce_fusion.2 = f32[12,12,128]{2,1,0:T(8,128)S(1)} fusion(f32[64]{0:T(128)S(1)} %copy-done.55, f32[12,12,128]{2,1,0:T(8,128)S(1)} %convert_multiply_fusion.2, f32[64]{0:T(128)S(1)} %get-tuple-element.310, f32[12,12,128]{2,1,0:T(8,128)S(1)} %subtract_multiply_fusion.10, f32[64]{0:T(128)S(1)} %get-tuple-element.311, ...), kind=kLoop, calls=%fused_computation.4 | loop fusion | flops 11778048 | bytes 370176 | tf_op jit(solution)/shard_map/reduce_sum | solution.py:76
  46.5 4.0 %multiply_reduce_fusion.6 = (f32[10,10,128]{2,1,0:T(8,128)}, f32[10,10,128]{2,1,0:T(8,128)S(1)}) fusion(f32[64]{0:T(128)S(1)} %copy-done.58, f32[64]{0:T(128)S(1)} %copy-done.55, f32[10,10,128]{2,1,0:T(8,128)S(1)} %convert_multiply_fusion.3, f32[64]{0:T(128)S(1)} %get-tuple-element.310, f32[10,10,128]{2,1,0:T(8,128)S(1)} %subtract_multiply_fusion.14, ...), kind=kLoop, calls=%fused_computation.18 | loop fusion | flops 15539200 | bytes 462336 | tf_op jit(solution)/shard_map/reduce_sum | solution.py:76
  50.6 0.7 fusion.167
  51.3 0.6 fusion.166
  52.0 0.6 fusion.13
  53.5 0.8 fusion.191
  54.3 1.9 %collective-permute-start.4 = (f32[5,8,1,128]{3,1,2,0:T(8,128)S(1)}, f32[5,8,1,128]{3,1,2,0:T(8,128)S(1)}, u32[]{:S(2)}, u32[]{:S(2)}) collective-permute-start(f32[5,8,1,128]{3,1,2,0:T(8,128)S(1)} %bitcast.159), channel_id=1, source_target_pairs={{0,1},{1,2},{2,3},{3,4},{4,5},{5,6},{6,7},{8,9},{9,10},{10,11},{11... | collective-permute-start | bytes 61448 | tf_op jit(solution)/shard_map/ppermute | solution.py:36
  56.2 6.0 %collective-permute-start.5 = (f32[5,8,1,128]{3,1,2,0:T(8,128)S(1)}, f32[5,8,1,128]{3,1,2,0:T(8,128)S(1)}, u32[]{:S(2)}, u32[]{:S(2)}) collective-permute-start(f32[5,8,1,128]{3,1,2,0:T(8,128)S(1)} %bitcast.158), channel_id=1, source_target_pairs={{1,0},{2,1},{3,2},{4,3},{5,4},{6,5},{7,6},{9,8},{10,9},{11,10},{12... | collective-permute-start | bytes 61448 | tf_op jit(solution)/shard_map/ppermute | solution.py:37
  62.2 1.4 collective-permute-start.7
  63.7 1.3 collective-permute-start.6
  65.5 0.6 slice_bitcast_fusion.17
  66.1 0.6 slice_bitcast_fusion.16
  67.1 0.7 fusion.171
  67.8 0.9 multiply_reduce_fusion.37
  69.3 4.6 %fusion.183 = (f32[64]{0:T(128)}, f32[8,8,128]{2,1,0:T(8,128)S(1)}, f32[8,8,128]{2,1,0:T(8,128)S(1)}, f32[64]{0:T(128)}, f32[64]{0:T(128)}, /*index=5*/f32[64]{0...) fusion(f32[64]{0:T(128)S(1)} %copy-done.55, ...), kind=kLoop, calls=%fused_computation.466 | loop fusion | flops 19889792 | bytes 396288 | tf_op jit(solution)/shard_map/reduce_sum | solution.py:170
  74.3 1.3 collective-permute-start.9
  75.6 5.4 %collective-permute-start.8 = (f32[5,2,8,128]{3,2,1,0:T(8,128)S(1)}, f32[5,2,8,128]{3,2,1,0:T(8,128)S(1)}, u32[]{:S(2)}, u32[]{:S(2)}) collective-permute-start(f32[5,2,8,128]{3,2,1,0:T(8,128)S(1)} %get-tuple-element.214), channel_id=1, source_target_pairs={{0,8},{8,16},{16,24},{24,32},{32,40},{40,48},{48,56},{56,64},{64,7... | collective-permute-start | bytes 122888 | tf_op jit(solution)/shard_map/ppermute | solution.py:20
  81.9 0.6 copy-done.13
  82.5 0.7 pad_maximum_fusion.48
  83.2 1.9 %collective-permute-start.11 = (f32[5,12,2,128]{3,2,1,0:T(2,128)}, f32[5,12,2,128]{3,2,1,0:T(2,128)}, u32[]{:S(2)}, u32[]{:S(2)}) collective-permute-start(f32[5,12,2,128]{3,2,1,0:T(2,128)} %get-tuple-element.188), channel_id=1, source_target_pairs={{1,0},{2,1},{3,2},{4,3},{5,4},{6,5},{7,6},{9,8},{10,9},{11,10},{12... | collective-permute-start | bytes 184328 | tf_op jit(solution)/shard_map/ppermute | solution.py:22
  85.1 3.9 %collective-permute-start.10 = (f32[5,12,2,128]{3,2,1,0:T(2,128)}, f32[5,12,2,128]{3,2,1,0:T(2,128)}, u32[]{:S(2)}, u32[]{:S(2)}) collective-permute-start(f32[5,12,2,128]{3,2,1,0:T(2,128)} %get-tuple-element.187), channel_id=1, source_target_pairs={{0,1},{1,2},{2,3},{3,4},{4,5},{5,6},{6,7},{8,9},{9,10},{10,11},{11... | collective-permute-start | bytes 184328 | tf_op jit(solution)/shard_map/ppermute | solution.py:20
  89.0 0.7 fusion.163
  89.7 0.7 concatenate.522
  90.5 3.2 %collective-permute-done.10 = f32[5,12,2,128]{3,2,1,0:T(2,128)} collective-permute-done((f32[5,12,2,128]{3,2,1,0:T(2,128)}, f32[5,12,2,128]{3,2,1,0:T(2,128)}, u32[]{:S(2)}, u32[]{:S(2)}) %collective-permute-start.10) | collective-permute-done | bytes 61472 | tf_op jit(solution)/shard_map/ppermute | solution.py:20
  93.6 1.0 pad_maximum_fusion.1
  95.6 1.2 multiply_reduce_fusion.41
  97.1 3.1 %multiply_reduce_fusion.5 = (f32[10,10,128]{2,1,0:T(8,128)S(1)}, f32[10,10,128]{2,1,0:T(8,128)S(1)}, f32[10,10,128]{2,1,0:T(8,128)S(1)}, f32[64,10,10,128]{3,0,2,1:T(8,128)S(1)}, f32[64,10,10,128]{3,0,2,1:T(8,128)S(1)}) fusion(f32[64]{0:T(128)S(1)} %get-tuple-element.308, f32[64]{0:T(128)S(1)} %copy-done.56, f32[10,10,128]{2,1,0:T(8,128)S(1)} %copy-done.23, ...), kind=kLoop, calls=%fused_computation.16 | loop fusion | flops 14707200 | bytes 6964736 | tf_op jit(solution)/shard_map/reduce_sum | solution.py:172
  100.4 1.3 multiply_add_fusion.5
  102.6 4.2 %fusion.184 = (f32[64]{0:T(128)S(1)}, f32[8,8,128]{2,1,0:T(8,128)S(1)}, f32[8,8,128]{2,1,0:T(8,128)S(1)}, f32[64]{0:T(128)S(1)}, f32[64]{0:T(128)S(1)}, /*index=...) fusion(f32[64]{0:T(128)S(1)} %copy-done.56, ...), kind=kLoop, calls=%fused_computation.467 | loop fusion | flops 19889792 | bytes 396288 | tf_op jit(solution)/shard_map/reduce_sum | solution.py:170
  107.4 1.9 %collective-permute-start.12 = (f32[5,8,1,128]{3,1,2,0:T(8,128)S(1)}, f32[5,8,1,128]{3,1,2,0:T(8,128)S(1)}, u32[]{:S(2)}, u32[]{:S(2)}) collective-permute-start(f32[5,8,1,128]{3,1,2,0:T(8,128)S(1)} %bitcast.161), channel_id=1, source_target_pairs={{0,1},{1,2},{2,3},{3,4},{4,5},{5,6},{6,7},{8,9},{9,10},{10,11},{11... | collective-permute-start | bytes 61448 | tf_op jit(solution)/shard_map/ppermute | solution.py:36
  109.3 6.0 %collective-permute-start.13 = (f32[5,8,1,128]{3,1,2,0:T(8,128)S(1)}, f32[5,8,1,128]{3,1,2,0:T(8,128)S(1)}, u32[]{:S(2)}, u32[]{:S(2)}) collective-permute-start(f32[5,8,1,128]{3,1,2,0:T(8,128)S(1)} %bitcast.160), channel_id=1, source_target_pairs={{1,0},{2,1},{3,2},{4,3},{5,4},{6,5},{7,6},{9,8},{10,9},{11,10},{12... | collective-permute-start | bytes 61448 | tf_op jit(solution)/shard_map/ppermute | solution.py:37
  115.3 2.2 %collective-permute-start.15 = (f32[5,1,8,128]{3,2,1,0:T(8,128)S(1)}, f32[5,1,8,128]{3,2,1,0:T(8,128)S(1)}, u32[]{:S(2)}, u32[]{:S(2)}) collective-permute-start(f32[5,1,8,128]{3,2,1,0:T(8,128)S(1)} %get-tuple-element.208), channel_id=1, source_target_pairs={{0,8},{8,16},{16,24},{24,32},{32,40},{40,48},{48,56},{56,64},{64,7... | collective-permute-start | bytes 61448 | tf_op jit(solution)/shard_map/ppermute | solution.py:36
  117.5 1.3 collective-permute-start.14
  118.9 1.0 slice_reduce_fusion
  120.6 3.5 %collective-permute-done.14 = f32[5,1,8,128]{3,2,1,0:T(8,128)S(1)} collective-permute-done((f32[5,1,8,128]{3,2,1,0:T(8,128)S(1)}, f32[5,1,8,128]{3,2,1,0:T(8,128)S(1)}, u32[]{:S(2)}, u32[]{:S(2)}) %collective-permute-start.14) | collective-permute-done | bytes 20512 | tf_op jit(solution)/shard_map/ppermute | solution.py:37
  124.4 3.1 %fusion.185 = (f32[64]{0:T(128)S(1)}, f32[8,8,128]{2,1,0:T(8,128)S(1)}, f32[8,8,128]{2,1,0:T(8,128)S(1)}, f32[64]{0:T(128)S(1)}, f32[64]{0:T(128)S(1)}, /*index=...) fusion(f32[64]{0:T(128)S(1)} %copy-done.57, f32[8,8,128]{2,1,0:T(8,128)S(1)} %copy-done.52, ...), kind=kLoop, calls=%fused_computation.468 | loop fusion | flops 15179392 | bytes 265216 | tf_op jit(solution)/shard_map/reduce_sum | solution.py:170
  127.6 3.6 %collective-permute-done.16 = f32[64,6]{0,1:T(8,128)S(1)} collective-permute-done((f32[64,6]{0,1:T(8,128)S(1)}, f32[64,6]{0,1:T(8,128)S(1)}, u32[]{:S(2)}, u32[]{:S(2)}) %collective-permute-start.16) | collective-permute-done | bytes 1568 | tf_op jit(solution)/shard_map/ppermute | solution.py:207
  131.2 5.1 %collective-permute-done.17 = f32[64,6]{0,1:T(8,128)S(1)} collective-permute-done((f32[64,6]{0,1:T(8,128)S(1)}, f32[64,6]{0,1:T(8,128)S(1)}, u32[]{:S(2)}, u32[]{:S(2)}) %collective-permute-start.17) | collective-permute-done | bytes 1568 | tf_op jit(solution)/shard_map/ppermute | solution.py:207
  136.3 3.6 %collective-permute-done.18 = f32[64,6]{0,1:T(8,128)S(1)} collective-permute-done((f32[64,6]{0,1:T(8,128)S(1)}, f32[64,6]{0,1:T(8,128)S(1)}, u32[]{:S(2)}, u32[]{:S(2)}) %collective-permute-start.18) | collective-permute-done | bytes 1568 | tf_op jit(solution)/shard_map/ppermute | solution.py:207
  139.9 1.2 collective-permute-done.19
  141.1 3.0 %collective-permute-start.20 = (f32[64,6]{0,1:T(8,128)S(1)}, f32[64,6]{0,1:T(8,128)S(1)}, u32[]{:S(2)}, u32[]{:S(2)}) collective-permute-start(f32[64,6]{0,1:T(8,128)S(1)} %add.898), channel_id=1, source_target_pairs={{0,16},{8,24},{16,0},{24,8},{32,48},{40,56},{48,32},{56,40},{64,80... | collective-permute-start | bytes 4616 | tf_op jit(solution)/shard_map/ppermute | solution.py:207
  144.4 1.3 collective-permute-done.20
  145.7 13.4 %collective-permute-start.21 = (f32[64,6]{0,1:T(8,128)S(1)}, f32[64,6]{0,1:T(8,128)S(1)}, u32[]{:S(2)}, u32[]{:S(2)}) collective-permute-start(f32[64,6]{0,1:T(8,128)S(1)} %add.899), channel_id=1, source_target_pairs={{0,32},{8,40},{16,48},{24,56},{32,0},{40,8},{48,16},{56,24},{64,96... | collective-permute-start | bytes 4616 | tf_op jit(solution)/shard_map/ppermute | solution.py:207
  159.1 1.6 collective-permute-done.21
  160.7 10.2 %collective-permute-start.22 = (f32[64,6]{0,1:T(8,128)S(1)}, f32[64,6]{0,1:T(8,128)S(1)}, u32[]{:S(2)}, u32[]{:S(2)}) collective-permute-start(f32[64,6]{0,1:T(8,128)S(1)} %add.900), channel_id=1, source_target_pairs={{0,64},{8,72},{16,80},{24,88},{32,96},{40,104},{48,112},{56,120},{... | collective-permute-start | bytes 4616 | tf_op jit(solution)/shard_map/ppermute | solution.py:207
  171.0 1.5 collective-permute-done.22
  172.5 8.1 %collective-permute-start.23 = (f32[64,6]{0,1:T(8,128)S(1)}, f32[64,6]{0,1:T(8,128)S(1)}, u32[]{:S(2)}, u32[]{:S(2)}) collective-permute-start(f32[64,6]{0,1:T(8,128)S(1)} %add.901), channel_id=1, source_target_pairs={{0,128},{8,136},{16,144},{24,152},{32,160},{40,168},{48,176},{56,1... | collective-permute-start | bytes 4616 | tf_op jit(solution)/shard_map/ppermute | solution.py:207
  180.7 1.5 collective-permute-done.23
  (288 shorter events, 16.6 us)
Async XLA Ops:
  0.6 11.6 %copy-start = (f32[5,8,8,128]{3,2,1,0:T(8,128)S(1)}, f32[5,8,8,128]{3,2,1,0:T(8,128)}, u32[]{:S(2)}) copy-start(f32[5,8,8,128]{3,2,1,0:T(8,128)} %param.15) | copy-start | bytes 491524
  2.4 16.2 %copy-start.54 = (f32[64,4]{0,1:T(4,128)S(1)}, f32[64,4]{0,1:T(4,128)}, u32[]{:S(2)}) copy-start(f32[64,4]{0,1:T(4,128)} %param.19) | copy-start | bytes 3076
  2.4 9.8 %collective-permute-start.1 = (f32[6,4,8,128]{3,2,1,0:T(8,128)S(1)}, f32[6,4,8,128]{3,2,1,0:T(8,128)S(1)}, u32[]{:S(2)}, u32[]{:S(2)}) collective-permute-start(f32[6,4,8,128]{3,2,1,0:T(8,128)S(1)} %get-tuple-element.202), channel_id=1, source_target_pairs={{8,0},{16,8},{24,16},{32,24},{40,32},{48,40},{56,48},{64,56},{72,6... | collective-permute-start | bytes 294920 | tf_op jit(solution)/shard_map/ppermute | solution.py:22
  3.7 8.5 %collective-permute-start = (f32[6,4,8,128]{3,2,1,0:T(8,128)S(1)}, f32[6,4,8,128]{3,2,1,0:T(8,128)S(1)}, u32[]{:S(2)}, u32[]{:S(2)}) collective-permute-start(f32[6,4,8,128]{3,2,1,0:T(8,128)S(1)} %get-tuple-element.201), channel_id=1, source_target_pairs={{0,8},{8,16},{16,24},{24,32},{32,40},{40,48},{48,56},{56,64},{64,7... | collective-permute-start | bytes 294920 | tf_op jit(solution)/shard_map/ppermute | solution.py:20
  12.4 9.4 %collective-permute-start.3 = (f32[6,16,4,128]{3,1,2,0:T(8,128)S(1)}, f32[6,16,4,128]{3,1,2,0:T(8,128)S(1)}, u32[]{:S(2)}, u32[]{:S(2)}) collective-permute-start(f32[6,16,4,128]{3,1,2,0:T(8,128)S(1)} %copy.262), channel_id=1, source_target_pairs={{1,0},{2,1},{3,2},{4,3},{5,4},{6,5},{7,6},{9,8},{10,9},{11,10},{12... | collective-permute-start | bytes 589832 | tf_op jit(solution)/shard_map/ppermute | solution.py:22
  16.6 11.7 %collective-permute-start.2 = (f32[6,16,4,128]{3,1,2,0:T(8,128)S(1)}, f32[6,16,4,128]{3,1,2,0:T(8,128)S(1)}, u32[]{:S(2)}, u32[]{:S(2)}) collective-permute-start(f32[6,16,4,128]{3,1,2,0:T(8,128)S(1)} %copy.261), channel_id=1, source_target_pairs={{0,1},{1,2},{2,3},{3,4},{4,5},{5,6},{6,7},{8,9},{9,10},{10,11},{11... | collective-permute-start | bytes 589832 | tf_op jit(solution)/shard_map/ppermute | solution.py:20
  45.3 5.1 %copy-start.22 = (f32[10,10,128]{2,1,0:T(8,128)}, f32[10,10,128]{2,1,0:T(8,128)S(1)}, u32[]{:S(2)}) copy-start(f32[10,10,128]{2,1,0:T(8,128)S(1)} %convert_multiply_fusion.3) | copy-start | bytes 153604
  46.0 35.0 %copy-start.15 = (f32[10,10,128]{2,1,0:T(8,128)}, f32[10,10,128]{2,1,0:T(8,128)S(1)}, u32[]{:S(2)}) copy-start(f32[10,10,128]{2,1,0:T(8,128)S(1)} %subtract_multiply_fusion.14) | copy-start | bytes 153604
  46.1 20.0 %copy-start.17 = (f32[10,10,128]{2,1,0:T(8,128)}, f32[10,10,128]{2,1,0:T(8,128)S(1)}, u32[]{:S(2)}) copy-start(f32[10,10,128]{2,1,0:T(8,128)S(1)} %subtract_multiply_fusion.15) | copy-start | bytes 153604
  46.2 19.3 %copy-start.19 = (f32[10,10,128]{2,1,0:T(8,128)}, f32[10,10,128]{2,1,0:T(8,128)S(1)}, u32[]{:S(2)}) copy-start(f32[10,10,128]{2,1,0:T(8,128)S(1)} %subtract_multiply_fusion.16) | copy-start | bytes 153604
  50.5 2.2 %copy-start.53 = (f32[5,256]{1,0:T(8,128)S(1)}, f32[5,256]{1,0:T(8,128)}, u32[]{:S(2)}) copy-start(f32[5,256]{1,0:T(8,128)} %param.18) | copy-start | bytes 15364
  54.3 14.6 %collective-permute-start.4 = (f32[5,8,1,128]{3,1,2,0:T(8,128)S(1)}, f32[5,8,1,128]{3,1,2,0:T(8,128)S(1)}, u32[]{:S(2)}, u32[]{:S(2)}) collective-permute-start(f32[5,8,1,128]{3,1,2,0:T(8,128)S(1)} %bitcast.159), channel_id=1, source_target_pairs={{0,1},{1,2},{2,3},{3,4},{4,5},{5,6},{6,7},{8,9},{9,10},{10,11},{11... | collective-permute-start | bytes 61448 | tf_op jit(solution)/shard_map/ppermute | solution.py:36
  56.2 12.7 %collective-permute-start.5 = (f32[5,8,1,128]{3,1,2,0:T(8,128)S(1)}, f32[5,8,1,128]{3,1,2,0:T(8,128)S(1)}, u32[]{:S(2)}, u32[]{:S(2)}) collective-permute-start(f32[5,8,1,128]{3,1,2,0:T(8,128)S(1)} %bitcast.158), channel_id=1, source_target_pairs={{1,0},{2,1},{3,2},{4,3},{5,4},{6,5},{7,6},{9,8},{10,9},{11,10},{12... | collective-permute-start | bytes 61448 | tf_op jit(solution)/shard_map/ppermute | solution.py:37
  62.2 6.9 %collective-permute-start.7 = (f32[5,1,8,128]{3,2,1,0:T(8,128)S(1)}, f32[5,1,8,128]{3,2,1,0:T(8,128)S(1)}, u32[]{:S(2)}, u32[]{:S(2)}) collective-permute-start(f32[5,1,8,128]{3,2,1,0:T(8,128)S(1)} %get-tuple-element.219), channel_id=1, source_target_pairs={{0,8},{8,16},{16,24},{24,32},{32,40},{40,48},{48,56},{56,64},{64,7... | collective-permute-start | bytes 61448 | tf_op jit(solution)/shard_map/ppermute | solution.py:36
  63.7 5.5 %collective-permute-start.6 = (f32[5,1,8,128]{3,2,1,0:T(8,128)S(1)}, f32[5,1,8,128]{3,2,1,0:T(8,128)S(1)}, u32[]{:S(2)}, u32[]{:S(2)}) collective-permute-start(f32[5,1,8,128]{3,2,1,0:T(8,128)S(1)} %get-tuple-element.218), channel_id=1, source_target_pairs={{8,0},{16,8},{24,16},{32,24},{40,32},{48,40},{56,48},{64,56},{72,6... | collective-permute-start | bytes 61448 | tf_op jit(solution)/shard_map/ppermute | solution.py:37
  65.0 4.3 %copy-start.51 = (f32[8,8,128]{2,1,0:T(8,128)}, f32[8,8,128]{2,1,0:T(8,128)S(1)}, u32[]{:S(2)}) copy-start(f32[8,8,128]{2,1,0:T(8,128)S(1)} %convert_multiply_fusion.4) | copy-start | bytes 98308
  67.0 2.2 %copy-start.45 = (f32[8,8,128]{2,1,0:T(8,128)}, f32[8,8,128]{2,1,0:T(8,128)S(1)}, u32[]{:S(2)}) copy-start(f32[8,8,128]{2,1,0:T(8,128)S(1)} %subtract_multiply_fusion.25) | copy-start | bytes 98308
  67.1 2.2 %copy-start.47 = (f32[8,8,128]{2,1,0:T(8,128)}, f32[8,8,128]{2,1,0:T(8,128)S(1)}, u32[]{:S(2)}) copy-start(f32[8,8,128]{2,1,0:T(8,128)S(1)} %subtract_multiply_fusion.26) | copy-start | bytes 98308
  68.9 5.0 %copy-start.49 = (f32[8,8,128]{2,1,0:T(8,128)}, f32[8,8,128]{2,1,0:T(8,128)S(1)}, u32[]{:S(2)}) copy-start(f32[8,8,128]{2,1,0:T(8,128)S(1)} %subtract_multiply_fusion.27) | copy-start | bytes 98308
  74.3 7.3 %collective-permute-start.9 = (f32[5,2,8,128]{3,2,1,0:T(8,128)S(1)}, f32[5,2,8,128]{3,2,1,0:T(8,128)S(1)}, u32[]{:S(2)}, u32[]{:S(2)}) collective-permute-start(f32[5,2,8,128]{3,2,1,0:T(8,128)S(1)} %get-tuple-element.215), channel_id=1, source_target_pairs={{8,0},{16,8},{24,16},{32,24},{40,32},{48,40},{56,48},{64,56},{72,6... | collective-permute-start | bytes 122888 | tf_op jit(solution)/shard_map/ppermute | solution.py:22
  75.6 6.2 %collective-permute-start.8 = (f32[5,2,8,128]{3,2,1,0:T(8,128)S(1)}, f32[5,2,8,128]{3,2,1,0:T(8,128)S(1)}, u32[]{:S(2)}, u32[]{:S(2)}) collective-permute-start(f32[5,2,8,128]{3,2,1,0:T(8,128)S(1)} %get-tuple-element.214), channel_id=1, source_target_pairs={{0,8},{8,16},{16,24},{24,32},{32,40},{40,48},{48,56},{56,64},{64,7... | collective-permute-start | bytes 122888 | tf_op jit(solution)/shard_map/ppermute | solution.py:20
  83.2 7.3 %collective-permute-start.11 = (f32[5,12,2,128]{3,2,1,0:T(2,128)}, f32[5,12,2,128]{3,2,1,0:T(2,128)}, u32[]{:S(2)}, u32[]{:S(2)}) collective-permute-start(f32[5,12,2,128]{3,2,1,0:T(2,128)} %get-tuple-element.188), channel_id=1, source_target_pairs={{1,0},{2,1},{3,2},{4,3},{5,4},{6,5},{7,6},{9,8},{10,9},{11,10},{12... | collective-permute-start | bytes 184328 | tf_op jit(solution)/shard_map/ppermute | solution.py:22
  85.1 8.5 %collective-permute-start.10 = (f32[5,12,2,128]{3,2,1,0:T(2,128)}, f32[5,12,2,128]{3,2,1,0:T(2,128)}, u32[]{:S(2)}, u32[]{:S(2)}) collective-permute-start(f32[5,12,2,128]{3,2,1,0:T(2,128)} %get-tuple-element.187), channel_id=1, source_target_pairs={{0,1},{1,2},{2,3},{3,4},{4,5},{5,6},{6,7},{8,9},{9,10},{10,11},{11... | collective-permute-start | bytes 184328 | tf_op jit(solution)/shard_map/ppermute | solution.py:20
  95.6 1.4 copy-start.23
  95.6 1.4 copy-start.56
  97.0 3.3 %copy-start.2 = (f32[10,10,128]{2,1,0:T(8,128)S(1)}, f32[10,10,128]{2,1,0:T(8,128)}, u32[]{:S(2)}) copy-start(f32[10,10,128]{2,1,0:T(8,128)} %copy-done.1) | copy-start | bytes 153604
  97.1 3.3 %copy-start.4 = (f32[10,10,128]{2,1,0:T(8,128)S(1)}, f32[10,10,128]{2,1,0:T(8,128)}, u32[]{:S(2)}) copy-start(f32[10,10,128]{2,1,0:T(8,128)} %copy-done.3) | copy-start | bytes 153604
  97.1 3.3 %copy-start.6 = (f32[10,10,128]{2,1,0:T(8,128)S(1)}, f32[10,10,128]{2,1,0:T(8,128)}, u32[]{:S(2)}) copy-start(f32[10,10,128]{2,1,0:T(8,128)} %copy-done.5) | copy-start | bytes 153604
  97.1 3.3 %copy-start.8 = (f32[10,10,128]{2,1,0:T(8,128)S(1)}, f32[10,10,128]{2,1,0:T(8,128)}, u32[]{:S(2)}) copy-start(f32[10,10,128]{2,1,0:T(8,128)} %copy-done.7) | copy-start | bytes 153604
  100.4 1.7 copy-start.9
  100.4 1.7 copy-start.10
  102.3 4.6 %copy-start.34 = (f32[8,8,128]{2,1,0:T(8,128)S(1)}, f32[8,8,128]{2,1,0:T(8,128)}, u32[]{:S(2)}) copy-start(f32[8,8,128]{2,1,0:T(8,128)} %get-tuple-element.240) | copy-start | bytes 98308
  102.3 4.6 %copy-start.35 = (f32[8,8,128]{2,1,0:T(8,128)S(1)}, f32[8,8,128]{2,1,0:T(8,128)}, u32[]{:S(2)}) copy-start(f32[8,8,128]{2,1,0:T(8,128)} %get-tuple-element.241) | copy-start | bytes 98308
  102.3 4.6 %copy-start.36 = (f32[8,8,128]{2,1,0:T(8,128)S(1)}, f32[8,8,128]{2,1,0:T(8,128)}, u32[]{:S(2)}) copy-start(f32[8,8,128]{2,1,0:T(8,128)} %get-tuple-element.242) | copy-start | bytes 98308
  102.3 4.6 %copy-start.37 = (f32[8,8,128]{2,1,0:T(8,128)S(1)}, f32[8,8,128]{2,1,0:T(8,128)}, u32[]{:S(2)}) copy-start(f32[8,8,128]{2,1,0:T(8,128)} %get-tuple-element.243) | copy-start | bytes 98308
  102.4 4.6 %copy-start.38 = (f32[8,8,128]{2,1,0:T(8,128)S(1)}, f32[8,8,128]{2,1,0:T(8,128)}, u32[]{:S(2)}) copy-start(f32[8,8,128]{2,1,0:T(8,128)} %get-tuple-element.244) | copy-start | bytes 98308
  102.4 4.6 %copy-start.39 = (f32[8,8,128]{2,1,0:T(8,128)S(1)}, f32[8,8,128]{2,1,0:T(8,128)}, u32[]{:S(2)}) copy-start(f32[8,8,128]{2,1,0:T(8,128)} %get-tuple-element.245) | copy-start | bytes 98308
  106.7 12.1 %copy-start.24 = (f32[8,8,128]{2,1,0:T(8,128)S(1)}, f32[8,8,128]{2,1,0:T(8,128)}, u32[]{:S(2)}) copy-start(f32[8,8,128]{2,1,0:T(8,128)} %slice_bitcast_fusion.17) | copy-start | bytes 98308
  106.7 12.1 %copy-start.25 = (f32[8,8,128]{2,1,0:T(8,128)S(1)}, f32[8,8,128]{2,1,0:T(8,128)}, u32[]{:S(2)}) copy-start(f32[8,8,128]{2,1,0:T(8,128)} %slice_bitcast_fusion.16) | copy-start | bytes 98308
  106.8 12.1 %copy-start.26 = (f32[8,8,128]{2,1,0:T(8,128)S(1)}, f32[8,8,128]{2,1,0:T(8,128)}, u32[]{:S(2)}) copy-start(f32[8,8,128]{2,1,0:T(8,128)} %slice_bitcast_fusion.15) | copy-start | bytes 98308
  106.8 12.1 %copy-start.27 = (f32[8,8,128]{2,1,0:T(8,128)S(1)}, f32[8,8,128]{2,1,0:T(8,128)}, u32[]{:S(2)}) copy-start(f32[8,8,128]{2,1,0:T(8,128)} %fusion.163) | copy-start | bytes 98308
  107.4 12.9 %collective-permute-start.12 = (f32[5,8,1,128]{3,1,2,0:T(8,128)S(1)}, f32[5,8,1,128]{3,1,2,0:T(8,128)S(1)}, u32[]{:S(2)}, u32[]{:S(2)}) collective-permute-start(f32[5,8,1,128]{3,1,2,0:T(8,128)S(1)} %bitcast.161), channel_id=1, source_target_pairs={{0,1},{1,2},{2,3},{3,4},{4,5},{5,6},{6,7},{8,9},{9,10},{10,11},{11... | collective-permute-start | bytes 61448 | tf_op jit(solution)/shard_map/ppermute | solution.py:36
  109.3 11.0 %collective-permute-start.13 = (f32[5,8,1,128]{3,1,2,0:T(8,128)S(1)}, f32[5,8,1,128]{3,1,2,0:T(8,128)S(1)}, u32[]{:S(2)}, u32[]{:S(2)}) collective-permute-start(f32[5,8,1,128]{3,1,2,0:T(8,128)S(1)} %bitcast.160), channel_id=1, source_target_pairs={{1,0},{2,1},{3,2},{4,3},{5,4},{6,5},{7,6},{9,8},{10,9},{11,10},{12... | collective-permute-start | bytes 61448 | tf_op jit(solution)/shard_map/ppermute | solution.py:37
  115.3 5.2 %collective-permute-start.15 = (f32[5,1,8,128]{3,2,1,0:T(8,128)S(1)}, f32[5,1,8,128]{3,2,1,0:T(8,128)S(1)}, u32[]{:S(2)}, u32[]{:S(2)}) collective-permute-start(f32[5,1,8,128]{3,2,1,0:T(8,128)S(1)} %get-tuple-element.208), channel_id=1, source_target_pairs={{0,8},{8,16},{16,24},{24,32},{32,40},{40,48},{48,56},{56,64},{64,7... | collective-permute-start | bytes 61448 | tf_op jit(solution)/shard_map/ppermute | solution.py:36
  117.5 6.6 %collective-permute-start.14 = (f32[5,1,8,128]{3,2,1,0:T(8,128)S(1)}, f32[5,1,8,128]{3,2,1,0:T(8,128)S(1)}, u32[]{:S(2)}, u32[]{:S(2)}) collective-permute-start(f32[5,1,8,128]{3,2,1,0:T(8,128)S(1)} %get-tuple-element.207), channel_id=1, source_target_pairs={{8,0},{16,8},{24,16},{32,24},{40,32},{48,40},{56,48},{64,56},{72,6... | collective-permute-start | bytes 61448 | tf_op jit(solution)/shard_map/ppermute | solution.py:37
  119.9 4.3 %copy-start.11 = (f32[5,8,8,127]{3,2,1,0:T(8,128)S(1)}, f32[5,8,8,127]{3,2,1,0:T(8,128)}, u32[]{:S(2)}) copy-start(f32[5,8,8,127]{3,2,1,0:T(8,128)} %get-tuple-element.203) | copy-start | bytes 487684
  119.9 4.3 %copy-start.12 = (f32[5,8,8,127]{3,2,1,0:T(8,128)S(1)}, f32[5,8,8,127]{3,2,1,0:T(8,128)}, u32[]{:S(2)}) copy-start(f32[5,8,8,127]{3,2,1,0:T(8,128)} %get-tuple-element.204) | copy-start | bytes 487684
  120.2 4.1 %copy-start.57 = (f32[64]{0:T(128)S(1)}, f32[64]{0:T(128)}, u32[]{:S(2)}) copy-start(f32[64]{0:T(128)} %param.20) | copy-start | bytes 772
  120.2 4.1 %copy-start.60 = (f32[64]{0:T(128)S(1)}, f32[64]{0:T(128)}, u32[]{:S(2)}) copy-start(f32[64]{0:T(128)} %param.21) | copy-start | bytes 772
  120.3 23.8 %copy-start.28 = (f32[8,8,128]{2,1,0:T(8,128)S(1)}, f32[8,8,128]{2,1,0:T(8,128)}, u32[]{:S(2)}) copy-start(f32[8,8,128]{2,1,0:T(8,128)} %get-tuple-element.116) | copy-start | bytes 98308
  120.3 23.8 %copy-start.29 = (f32[8,8,128]{2,1,0:T(8,128)S(1)}, f32[8,8,128]{2,1,0:T(8,128)}, u32[]{:S(2)}) copy-start(f32[8,8,128]{2,1,0:T(8,128)} %get-tuple-element.171) | copy-start | bytes 98308
  120.3 23.8 %copy-start.30 = (f32[8,8,128]{2,1,0:T(8,128)S(1)}, f32[8,8,128]{2,1,0:T(8,128)}, u32[]{:S(2)}) copy-start(f32[8,8,128]{2,1,0:T(8,128)} %get-tuple-element.173) | copy-start | bytes 98308
  120.4 23.8 %copy-start.31 = (f32[8,8,128]{2,1,0:T(8,128)S(1)}, f32[8,8,128]{2,1,0:T(8,128)}, u32[]{:S(2)}) copy-start(f32[8,8,128]{2,1,0:T(8,128)} %get-tuple-element.175) | copy-start | bytes 98308
  120.4 23.8 %copy-start.32 = (f32[8,8,128]{2,1,0:T(8,128)S(1)}, f32[8,8,128]{2,1,0:T(8,128)}, u32[]{:S(2)}) copy-start(f32[8,8,128]{2,1,0:T(8,128)} %get-tuple-element.118) | copy-start | bytes 98308
  120.4 23.8 %copy-start.33 = (f32[8,8,128]{2,1,0:T(8,128)S(1)}, f32[8,8,128]{2,1,0:T(8,128)}, u32[]{:S(2)}) copy-start(f32[8,8,128]{2,1,0:T(8,128)} %get-tuple-element.177) | copy-start | bytes 98308
  127.5 3.7 %collective-permute-start.16 = (f32[64,6]{0,1:T(8,128)S(1)}, f32[64,6]{0,1:T(8,128)S(1)}, u32[]{:S(2)}, u32[]{:S(2)}) collective-permute-start(f32[64,6]{0,1:T(8,128)S(1)} %add_add_fusion), channel_id=1, source_target_pairs={{0,1},{1,0},{2,3},{3,2},{4,5},{5,4},{6,7},{7,6},{8,9},{9,8},{10,11... | collective-permute-start | bytes 4616 | tf_op jit(solution)/shard_map/ppermute | solution.py:207
  131.2 5.1 %collective-permute-start.17 = (f32[64,6]{0,1:T(8,128)S(1)}, f32[64,6]{0,1:T(8,128)S(1)}, u32[]{:S(2)}, u32[]{:S(2)}) collective-permute-start(f32[64,6]{0,1:T(8,128)S(1)} %add.895), channel_id=1, source_target_pairs={{0,2},{1,3},{2,0},{3,1},{4,6},{5,7},{6,4},{7,5},{8,10},{9,11},{10,... | collective-permute-start | bytes 4616 | tf_op jit(solution)/shard_map/ppermute | solution.py:207
  136.3 3.6 %collective-permute-start.18 = (f32[64,6]{0,1:T(8,128)S(1)}, f32[64,6]{0,1:T(8,128)S(1)}, u32[]{:S(2)}, u32[]{:S(2)}) collective-permute-start(f32[64,6]{0,1:T(8,128)S(1)} %add.896), channel_id=1, source_target_pairs={{0,4},{1,5},{2,6},{3,7},{4,0},{5,1},{6,2},{7,3},{8,12},{9,13},{10,... | collective-permute-start | bytes 4616 | tf_op jit(solution)/shard_map/ppermute | solution.py:207
  139.9 1.2 collective-permute-start.19
  141.1 4.6 %collective-permute-start.20 = (f32[64,6]{0,1:T(8,128)S(1)}, f32[64,6]{0,1:T(8,128)S(1)}, u32[]{:S(2)}, u32[]{:S(2)}) collective-permute-start(f32[64,6]{0,1:T(8,128)S(1)} %add.898), channel_id=1, source_target_pairs={{0,16},{8,24},{16,0},{24,8},{32,48},{40,56},{48,32},{56,40},{64,80... | collective-permute-start | bytes 4616 | tf_op jit(solution)/shard_map/ppermute | solution.py:207
  145.7 15.0 %collective-permute-start.21 = (f32[64,6]{0,1:T(8,128)S(1)}, f32[64,6]{0,1:T(8,128)S(1)}, u32[]{:S(2)}, u32[]{:S(2)}) collective-permute-start(f32[64,6]{0,1:T(8,128)S(1)} %add.899), channel_id=1, source_target_pairs={{0,32},{8,40},{16,48},{24,56},{32,0},{40,8},{48,16},{56,24},{64,96... | collective-permute-start | bytes 4616 | tf_op jit(solution)/shard_map/ppermute | solution.py:207
  160.7 11.8 %collective-permute-start.22 = (f32[64,6]{0,1:T(8,128)S(1)}, f32[64,6]{0,1:T(8,128)S(1)}, u32[]{:S(2)}, u32[]{:S(2)}) collective-permute-start(f32[64,6]{0,1:T(8,128)S(1)} %add.900), channel_id=1, source_target_pairs={{0,64},{8,72},{16,80},{24,88},{32,96},{40,104},{48,112},{56,120},{... | collective-permute-start | bytes 4616 | tf_op jit(solution)/shard_map/ppermute | solution.py:207
  172.5 9.6 %collective-permute-start.23 = (f32[64,6]{0,1:T(8,128)S(1)}, f32[64,6]{0,1:T(8,128)S(1)}, u32[]{:S(2)}, u32[]{:S(2)}) collective-permute-start(f32[64,6]{0,1:T(8,128)S(1)} %add.901), channel_id=1, source_target_pairs={{0,128},{8,136},{16,144},{24,152},{32,160},{40,168},{48,176},{56,1... | collective-permute-start | bytes 4616 | tf_op jit(solution)/shard_map/ppermute | solution.py:207
  180.7 2.1 %copy-start.21 = (f32[5,8,8,128]{3,2,1,0:T(8,128)}, f32[5,8,8,128]{3,2,1,0:T(8,128)S(1)}, u32[]{:S(2)}) copy-start(f32[5,8,8,128]{3,2,1,0:T(8,128)S(1)} %fusion.133) | copy-start | bytes 491524
  (21 other events, 20.5 us)
where the time goes:
time: 184 us; the launch traced here: 183 us
  starting transfers between devices  79.8 us (43%)
  other arithmetic  50.5 us (27%)
  waiting for transfers between devices  36 us (20%)
  local copies, waits for them, and re-layouts  13 us (7%)
  between operations  2.36 us (1%)
    ppermute x8, starting transfers between devices, butterfly_sum(): lax.ppermute(values, axis, [(i, i ^ step) for i in range(count)])  34.8 us
    ppermute x8, waiting for transfers between devices, butterfly_sum(): lax.ppermute(values, axis, [(i, i ^ step) for i in range(count)])  19.4 us
    ppermute x4, starting transfers between devices, faces_padded(): lax.ppermute(head, axis, [((i + 1) % count, i) for i in range(ends)])  14.6 us
    reduce_sum x5, other arithmetic, logit_of(): return jnp.sum(spread(w_out, hidden.ndim - 1) * hidden, axis=0)  14.5 us
    ppermute x4, starting transfers between devices, padded_2(): lax.ppermute(tail, axis, [(i, (i + 1) % count) for i in range(ends)])  14.2 us
    reduce_sum x4, other arithmetic, adjoint_step(): bias_grad = jnp.sum(before_core, axis=cells)  12.8 us
    ppermute x4, waiting for transfers between devices, padded_2(): lax.ppermute(tail, axis, [(i, (i + 1) % count) for i in range(ends)])  9.87 us
    ppermute x4, starting transfers between devices, padded_2(): lax.ppermute(head, axis, [((i + 1) % count, i) for i in range(ends)])  8.71 us
  transfers between devices with their start and end apart: 24, of which 13 were waited for; matrix products, arithmetic and copies ran while one was open for 8% of the time, Pallas kernels for 0%

commit v1 on v0

--- a/solution.py
+++ b/solution.py
@@ -37,12 +37,8 @@
         parts.append(lax.ppermute(head, axis, [((i + 1) % count, i) for i in range(ends)]))
     low_x, high_x, low_y, high_y = parts
     middle = jnp.concatenate([low_y, cells, high_y], axis=2)
-    shape = list(low_x.shape)
-    shape[2] = width
-    blank = jnp.zeros(shape, cells.dtype)
-    low_x = jnp.concatenate([blank, low_x, blank], axis=2)
-    high_x = jnp.concatenate([blank, high_x, blank], axis=2)
-    return jnp.concatenate([low_x, middle, high_x], axis=1)
+    edge = ((0, 0), (0, 0), (width, width), (0, 0))
+    return jnp.concatenate([jnp.pad(low_x, edge), middle, jnp.pad(high_x, edge)], axis=1)
 
 
 def vertical_diff(values):

time: 184 us -> 184 us (level)
  transfers between devices with their start and end apart: 24 -> 24, of which waited for: 13 -> 13; matrix products, arithmetic and copies ran while one was open for 8% -> 7% of each run, Pallas kernels for 0% -> 0%
where the time goes in v1:
time: 184 us; the launch traced here: 183 us
  starting transfers between devices  79.8 us (43%)
  other arithmetic  50.6 us (28%)
  waiting for transfers between devices  36.1 us (20%)
  local copies, waits for them, and re-layouts  12.9 us (7%)
  between operations  2.31 us (1%)
    ppermute x8, starting transfers between devices, butterfly_sum(): lax.ppermute(values, axis, [(i, i ^ step) for i in range(count)])  34.8 us
    ppermute x8, waiting for transfers between devices, butterfly_sum(): lax.ppermute(values, axis, [(i, i ^ step) for i in range(count)])  19.4 us
    ppermute x4, starting transfers between devices, faces_padded(): lax.ppermute(head, axis, [((i + 1) % count, i) for i in range(ends)])  14.6 us
    reduce_sum x5, other arithmetic, logit_of(): return jnp.sum(spread(w_out, hidden.ndim - 1) * hidden, axis=0)  14.5 us
    ppermute x4, starting transfers between devices, padded_2(): lax.ppermute(tail, axis, [(i, (i + 1) % count) for i in range(ends)])  14.2 us
    reduce_sum x4, other arithmetic, adjoint_step(): bias_grad = jnp.sum(before_core, axis=cells)  12.9 us
    ppermute x4, waiting for transfers between devices, padded_2(): lax.ppermute(tail, axis, [(i, (i + 1) % count) for i in range(ends)])  9.87 us
    ppermute x4, starting transfers between devices, padded_2(): lax.ppermute(head, axis, [((i + 1) % count, i) for i in range(ends)])  8.71 us
  transfers between devices with their start and end apart: 24, of which 13 were waited for; matrix products, arithmetic and copies ran while one was open for 7% of the time, Pallas kernels for 0%

profile of v1, /device:TPU:32, one launch (start us, length us, event | category | flops | bytes accessed | tf_op | source)
XLA Modules:
  0.0 182.8 jit_solution(8689188836149061951)
XLA Ops:
  0.6 0.7 subtract_convert_fusion
  1.4 0.9 fusion.132
  2.4 1.3 collective-permute-start.1
  3.7 3.0 %collective-permute-start = (f32[6,4,8,128]{3,2,1,0:T(8,128)S(1)}, f32[6,4,8,128]{3,2,1,0:T(8,128)S(1)}, u32[]{:S(2)}, u32[]{:S(2)}) collective-permute-start(f32[6,4,8,128]{3,2,1,0:T(8,128)S(1)} %get-tuple-element.202), channel_id=1, source_target_pairs={{0,8},{8,16},{16,24},{24,32},{32,40},{40,48},{48,56},{56,64},{64,7... | collective-permute-start | bytes 294920 | tf_op jit(solution)/shard_map/ppermute | solution.py:20
  6.7 0.8 slice_bitcast_fusion.26
  7.6 1.8 fusion.199
  9.3 0.7 and_select_fusion.1
  10.1 0.7 subtract_multiply_fusion.21
  10.9 0.7 subtract_multiply_fusion.22
  11.5 0.7 subtract_multiply_fusion.23
  12.4 4.2 %collective-permute-start.3 = (f32[6,16,4,128]{3,1,2,0:T(8,128)S(1)}, f32[6,16,4,128]{3,1,2,0:T(8,128)S(1)}, u32[]{:S(2)}, u32[]{:S(2)}) collective-permute-start(f32[6,16,4,128]{3,1,2,0:T(8,128)S(1)} %copy.254), channel_id=1, source_target_pairs={{1,0},{2,1},{3,2},{4,3},{5,4},{6,5},{7,6},{9,8},{10,9},{11,10},{12... | collective-permute-start | bytes 589832 | tf_op jit(solution)/shard_map/ppermute | solution.py:22
  16.6 1.9 %collective-permute-start.2 = (f32[6,16,4,128]{3,1,2,0:T(8,128)S(1)}, f32[6,16,4,128]{3,1,2,0:T(8,128)S(1)}, u32[]{:S(2)}, u32[]{:S(2)}) collective-permute-start(f32[6,16,4,128]{3,1,2,0:T(8,128)S(1)} %copy.253), channel_id=1, source_target_pairs={{0,1},{1,2},{2,3},{3,4},{4,5},{5,6},{6,7},{8,9},{9,10},{10,11},{11... | collective-permute-start | bytes 589832 | tf_op jit(solution)/shard_map/ppermute | solution.py:20
  18.6 3.3 %collective-permute-done.3 = f32[6,16,4,128]{3,1,2,0:T(8,128)S(1)} collective-permute-done((f32[6,16,4,128]{3,1,2,0:T(8,128)S(1)}, f32[6,16,4,128]{3,1,2,0:T(8,128)S(1)}, u32[]{:S(2)}, u32[]{:S(2)}) %collective-permute-start.3) | collective-permute-done | bytes 196640 | tf_op jit(solution)/shard_map/ppermute | solution.py:22
  21.9 6.4 %collective-permute-done.2 = f32[6,16,4,128]{3,1,2,0:T(8,128)S(1)} collective-permute-done((f32[6,16,4,128]{3,1,2,0:T(8,128)S(1)}, f32[6,16,4,128]{3,1,2,0:T(8,128)S(1)}, u32[]{:S(2)}, u32[]{:S(2)}) %collective-permute-start.2) | collective-permute-done | bytes 196640 | tf_op jit(solution)/shard_map/ppermute | solution.py:20
  30.0 3.7 %multiply_reduce_fusion = f32[16,16,128]{2,1,0:T(8,128)S(1)} fusion(f32[64]{0:T(128)S(1)} %copy-done.55, f32[16,16,128]{2,1,0:T(8,128)S(1)} %get-tuple-element.317, f32[64]{0:T(128)S(1)} %get-tuple-element.311, f32[16,16,128]{2,1,0:T(8,128)S(1)} %get-tuple-element.318, f32[64]{0:T(128)S(1)} %get-tuple-element.312, ...), kind=kLoop, calls=%fused_computation | loop fusion | flops 20938752 | bytes 656896 | tf_op jit(solution)/shard_map/reduce_sum | solution.py:72
  35.9 3.6 %multiply_reduce_fusion.1 = f32[14,14,128]{2,1,0:T(8,128)S(1)} fusion(f32[64]{0:T(128)S(1)} %copy-done.55, f32[14,14,128]{2,1,0:T(8,128)S(1)} %convert_multiply_fusion.1, f32[64]{0:T(128)S(1)} %get-tuple-element.311, f32[14,14,128]{2,1,0:T(8,128)S(1)} %subtract_multiply_fusion.7, f32[64]{0:T(128)S(1)} %get-tuple-element.312, ...), kind=kLoop, calls=%fused_computation.1 | loop fusion | flops 16031232 | bytes 503296 | tf_op jit(solution)/shard_map/reduce_sum | solution.py:72
  41.4 2.3 %multiply_reduce_fusion.2 = f32[12,12,128]{2,1,0:T(8,128)S(1)} fusion(f32[64]{0:T(128)S(1)} %copy-done.55, f32[12,12,128]{2,1,0:T(8,128)S(1)} %convert_multiply_fusion.2, f32[64]{0:T(128)S(1)} %get-tuple-element.311, f32[12,12,128]{2,1,0:T(8,128)S(1)} %subtract_multiply_fusion.10, f32[64]{0:T(128)S(1)} %get-tuple-element.312, ...), kind=kLoop, calls=%fused_computation.4 | loop fusion | flops 11778048 | bytes 370176 | tf_op jit(solution)/shard_map/reduce_sum | solution.py:72
  46.5 4.0 %multiply_reduce_fusion.6 = (f32[10,10,128]{2,1,0:T(8,128)}, f32[10,10,128]{2,1,0:T(8,128)S(1)}) fusion(f32[64]{0:T(128)S(1)} %copy-done.56, f32[64]{0:T(128)S(1)} %copy-done.55, f32[10,10,128]{2,1,0:T(8,128)S(1)} %convert_multiply_fusion.3, f32[64]{0:T(128)S(1)} %get-tuple-element.311, f32[10,10,128]{2,1,0:T(8,128)S(1)} %subtract_multiply_fusion.14, ...), kind=kLoop, calls=%fused_computation.18 | loop fusion | flops 15539200 | bytes 462336 | tf_op jit(solution)/shard_map/reduce_sum | solution.py:72
  50.6 0.7 fusion.167
  51.3 0.6 fusion.166
  52.0 0.6 fusion.13
  53.5 0.8 fusion.191
  54.3 1.9 %collective-permute-start.4 = (f32[5,8,1,128]{3,1,2,0:T(8,128)S(1)}, f32[5,8,1,128]{3,1,2,0:T(8,128)S(1)}, u32[]{:S(2)}, u32[]{:S(2)}) collective-permute-start(f32[5,8,1,128]{3,1,2,0:T(8,128)S(1)} %bitcast.155), channel_id=1, source_target_pairs={{0,1},{1,2},{2,3},{3,4},{4,5},{5,6},{6,7},{8,9},{9,10},{10,11},{11... | collective-permute-start | bytes 61448 | tf_op jit(solution)/shard_map/ppermute | solution.py:36
  56.2 6.0 %collective-permute-start.5 = (f32[5,8,1,128]{3,1,2,0:T(8,128)S(1)}, f32[5,8,1,128]{3,1,2,0:T(8,128)S(1)}, u32[]{:S(2)}, u32[]{:S(2)}) collective-permute-start(f32[5,8,1,128]{3,1,2,0:T(8,128)S(1)} %bitcast.156), channel_id=1, source_target_pairs={{1,0},{2,1},{3,2},{4,3},{5,4},{6,5},{7,6},{9,8},{10,9},{11,10},{12... | collective-permute-start | bytes 61448 | tf_op jit(solution)/shard_map/ppermute | solution.py:37
  62.2 1.4 collective-permute-start.7
  63.6 1.3 collective-permute-start.6
  65.5 0.6 slice_bitcast_fusion.17
  66.1 0.6 slice_bitcast_fusion.16
  67.1 0.7 fusion.171
  67.8 1.0 multiply_reduce_fusion.37
  69.3 4.6 %fusion.183 = (f32[64]{0:T(128)}, f32[8,8,128]{2,1,0:T(8,128)S(1)}, f32[8,8,128]{2,1,0:T(8,128)S(1)}, f32[64]{0:T(128)}, f32[64]{0:T(128)}, /*index=5*/f32[64]{0...) fusion(f32[64]{0:T(128)S(1)} %copy-done.55, ...), kind=kLoop, calls=%fused_computation.464 | loop fusion | flops 19889792 | bytes 396288 | tf_op jit(solution)/shard_map/reduce_sum | solution.py:166
  74.3 1.3 collective-permute-start.9
  75.6 5.4 %collective-permute-start.8 = (f32[5,2,8,128]{3,2,1,0:T(8,128)S(1)}, f32[5,2,8,128]{3,2,1,0:T(8,128)S(1)}, u32[]{:S(2)}, u32[]{:S(2)}) collective-permute-start(f32[5,2,8,128]{3,2,1,0:T(8,128)S(1)} %get-tuple-element.215), channel_id=1, source_target_pairs={{0,8},{8,16},{16,24},{24,32},{32,40},{40,48},{48,56},{56,64},{64,7... | collective-permute-start | bytes 122888 | tf_op jit(solution)/shard_map/ppermute | solution.py:20
  81.8 0.6 copy-done.13
  82.5 0.7 pad_maximum_fusion.40
  83.2 1.9 %collective-permute-start.11 = (f32[5,12,2,128]{3,2,1,0:T(2,128)}, f32[5,12,2,128]{3,2,1,0:T(2,128)}, u32[]{:S(2)}, u32[]{:S(2)}) collective-permute-start(f32[5,12,2,128]{3,2,1,0:T(2,128)} %get-tuple-element.189), channel_id=1, source_target_pairs={{1,0},{2,1},{3,2},{4,3},{5,4},{6,5},{7,6},{9,8},{10,9},{11,10},{12... | collective-permute-start | bytes 184328 | tf_op jit(solution)/shard_map/ppermute | solution.py:22
  85.1 3.9 %collective-permute-start.10 = (f32[5,12,2,128]{3,2,1,0:T(2,128)}, f32[5,12,2,128]{3,2,1,0:T(2,128)}, u32[]{:S(2)}, u32[]{:S(2)}) collective-permute-start(f32[5,12,2,128]{3,2,1,0:T(2,128)} %get-tuple-element.188), channel_id=1, source_target_pairs={{0,1},{1,2},{2,3},{3,4},{4,5},{5,6},{6,7},{8,9},{9,10},{10,11},{11... | collective-permute-start | bytes 184328 | tf_op jit(solution)/shard_map/ppermute | solution.py:20
  89.0 0.7 fusion.163
  89.7 0.7 concatenate.506
  90.4 3.2 %collective-permute-done.10 = f32[5,12,2,128]{3,2,1,0:T(2,128)} collective-permute-done((f32[5,12,2,128]{3,2,1,0:T(2,128)}, f32[5,12,2,128]{3,2,1,0:T(2,128)}, u32[]{:S(2)}, u32[]{:S(2)}) %collective-permute-start.10) | collective-permute-done | bytes 61472 | tf_op jit(solution)/shard_map/ppermute | solution.py:20
  93.6 1.0 pad_maximum_fusion.1
  95.6 1.2 multiply_reduce_fusion.41
  97.0 3.1 %multiply_reduce_fusion.5 = (f32[10,10,128]{2,1,0:T(8,128)S(1)}, f32[10,10,128]{2,1,0:T(8,128)S(1)}, f32[10,10,128]{2,1,0:T(8,128)S(1)}, f32[64,10,10,128]{3,0,2,1:T(8,128)S(1)}, f32[64,10,10,128]{3,0,2,1:T(8,128)S(1)}) fusion(f32[64]{0:T(128)S(1)} %get-tuple-element.309, f32[64]{0:T(128)S(1)} %copy-done.55, f32[10,10,128]{2,1,0:T(8,128)S(1)} %copy-done.23, ...), kind=kLoop, calls=%fused_computation.16 | loop fusion | flops 14707200 | bytes 6964736 | tf_op jit(solution)/shard_map/reduce_sum | solution.py:168
  100.4 1.3 multiply_add_fusion.5
  102.5 4.2 %fusion.184 = (f32[64]{0:T(128)S(1)}, f32[8,8,128]{2,1,0:T(8,128)S(1)}, f32[8,8,128]{2,1,0:T(8,128)S(1)}, f32[64]{0:T(128)S(1)}, f32[64]{0:T(128)S(1)}, /*index=...) fusion(f32[64]{0:T(128)S(1)} %copy-done.55, ...), kind=kLoop, calls=%fused_computation.465 | loop fusion | flops 19889792 | bytes 396288 | tf_op jit(solution)/shard_map/reduce_sum | solution.py:166
  107.3 1.9 %collective-permute-start.12 = (f32[5,8,1,128]{3,1,2,0:T(8,128)S(1)}, f32[5,8,1,128]{3,1,2,0:T(8,128)S(1)}, u32[]{:S(2)}, u32[]{:S(2)}) collective-permute-start(f32[5,8,1,128]{3,1,2,0:T(8,128)S(1)} %bitcast.158), channel_id=1, source_target_pairs={{0,1},{1,2},{2,3},{3,4},{4,5},{5,6},{6,7},{8,9},{9,10},{10,11},{11... | collective-permute-start | bytes 61448 | tf_op jit(solution)/shard_map/ppermute | solution.py:36
  109.3 6.0 %collective-permute-start.13 = (f32[5,8,1,128]{3,1,2,0:T(8,128)S(1)}, f32[5,8,1,128]{3,1,2,0:T(8,128)S(1)}, u32[]{:S(2)}, u32[]{:S(2)}) collective-permute-start(f32[5,8,1,128]{3,1,2,0:T(8,128)S(1)} %bitcast.157), channel_id=1, source_target_pairs={{1,0},{2,1},{3,2},{4,3},{5,4},{6,5},{7,6},{9,8},{10,9},{11,10},{12... | collective-permute-start | bytes 61448 | tf_op jit(solution)/shard_map/ppermute | solution.py:37
  115.3 2.2 %collective-permute-start.15 = (f32[5,1,8,128]{3,2,1,0:T(8,128)S(1)}, f32[5,1,8,128]{3,2,1,0:T(8,128)S(1)}, u32[]{:S(2)}, u32[]{:S(2)}) collective-permute-start(f32[5,1,8,128]{3,2,1,0:T(8,128)S(1)} %get-tuple-element.209), channel_id=1, source_target_pairs={{0,8},{8,16},{16,24},{24,32},{32,40},{40,48},{48,56},{56,64},{64,7... | collective-permute-start | bytes 61448 | tf_op jit(solution)/shard_map/ppermute | solution.py:36
  117.5 1.3 collective-permute-start.14
  118.8 1.0 slice_reduce_fusion
  120.6 3.6 %collective-permute-done.14 = f32[5,1,8,128]{3,2,1,0:T(8,128)S(1)} collective-permute-done((f32[5,1,8,128]{3,2,1,0:T(8,128)S(1)}, f32[5,1,8,128]{3,2,1,0:T(8,128)S(1)}, u32[]{:S(2)}, u32[]{:S(2)}) %collective-permute-start.14) | collective-permute-done | bytes 20512 | tf_op jit(solution)/shard_map/ppermute | solution.py:37
  124.3 3.1 %fusion.185 = (f32[64]{0:T(128)S(1)}, f32[8,8,128]{2,1,0:T(8,128)S(1)}, f32[8,8,128]{2,1,0:T(8,128)S(1)}, f32[64]{0:T(128)S(1)}, f32[64]{0:T(128)S(1)}, /*index=...) fusion(f32[64]{0:T(128)S(1)} %copy-done.55, f32[8,8,128]{2,1,0:T(8,128)S(1)} %copy-done.52, ...), kind=kLoop, calls=%fused_computation.466 | loop fusion | flops 15179392 | bytes 265216 | tf_op jit(solution)/shard_map/reduce_sum | solution.py:166
  127.6 3.6 %collective-permute-done.16 = f32[64,6]{0,1:T(8,128)S(1)} collective-permute-done((f32[64,6]{0,1:T(8,128)S(1)}, f32[64,6]{0,1:T(8,128)S(1)}, u32[]{:S(2)}, u32[]{:S(2)}) %collective-permute-start.16) | collective-permute-done | bytes 1568 | tf_op jit(solution)/shard_map/ppermute | solution.py:203
  131.2 5.1 %collective-permute-done.17 = f32[64,6]{0,1:T(8,128)S(1)} collective-permute-done((f32[64,6]{0,1:T(8,128)S(1)}, f32[64,6]{0,1:T(8,128)S(1)}, u32[]{:S(2)}, u32[]{:S(2)}) %collective-permute-start.17) | collective-permute-done | bytes 1568 | tf_op jit(solution)/shard_map/ppermute | solution.py:203
  136.3 3.6 %collective-permute-done.18 = f32[64,6]{0,1:T(8,128)S(1)} collective-permute-done((f32[64,6]{0,1:T(8,128)S(1)}, f32[64,6]{0,1:T(8,128)S(1)}, u32[]{:S(2)}, u32[]{:S(2)}) %collective-permute-start.18) | collective-permute-done | bytes 1568 | tf_op jit(solution)/shard_map/ppermute | solution.py:203
  139.9 1.2 collective-permute-done.19
  141.1 2.9 %collective-permute-start.20 = (f32[64,6]{0,1:T(8,128)S(1)}, f32[64,6]{0,1:T(8,128)S(1)}, u32[]{:S(2)}, u32[]{:S(2)}) collective-permute-start(f32[64,6]{0,1:T(8,128)S(1)} %add.906), channel_id=1, source_target_pairs={{0,16},{8,24},{16,0},{24,8},{32,48},{40,56},{48,32},{56,40},{64,80... | collective-permute-start | bytes 4616 | tf_op jit(solution)/shard_map/ppermute | solution.py:203
  144.3 1.4 collective-permute-done.20
  145.6 13.5 %collective-permute-start.21 = (f32[64,6]{0,1:T(8,128)S(1)}, f32[64,6]{0,1:T(8,128)S(1)}, u32[]{:S(2)}, u32[]{:S(2)}) collective-permute-start(f32[64,6]{0,1:T(8,128)S(1)} %add.907), channel_id=1, source_target_pairs={{0,32},{8,40},{16,48},{24,56},{32,0},{40,8},{48,16},{56,24},{64,96... | collective-permute-start | bytes 4616 | tf_op jit(solution)/shard_map/ppermute | solution.py:203
  159.2 1.6 collective-permute-done.21
  160.8 10.2 %collective-permute-start.22 = (f32[64,6]{0,1:T(8,128)S(1)}, f32[64,6]{0,1:T(8,128)S(1)}, u32[]{:S(2)}, u32[]{:S(2)}) collective-permute-start(f32[64,6]{0,1:T(8,128)S(1)} %add.908), channel_id=1, source_target_pairs={{0,64},{8,72},{16,80},{24,88},{32,96},{40,104},{48,112},{56,120},{... | collective-permute-start | bytes 4616 | tf_op jit(solution)/shard_map/ppermute | solution.py:203
  171.1 1.5 collective-permute-done.22
  172.6 8.0 %collective-permute-start.23 = (f32[64,6]{0,1:T(8,128)S(1)}, f32[64,6]{0,1:T(8,128)S(1)}, u32[]{:S(2)}, u32[]{:S(2)}) collective-permute-start(f32[64,6]{0,1:T(8,128)S(1)} %add.909), channel_id=1, source_target_pairs={{0,128},{8,136},{16,144},{24,152},{32,160},{40,168},{48,176},{56,1... | collective-permute-start | bytes 4616 | tf_op jit(solution)/shard_map/ppermute | solution.py:203
  180.7 1.5 collective-permute-done.23
  (282 shorter events, 16.6 us)
Async XLA Ops:
  0.6 11.6 %copy-start = (f32[5,8,8,128]{3,2,1,0:T(8,128)S(1)}, f32[5,8,8,128]{3,2,1,0:T(8,128)}, u32[]{:S(2)}) copy-start(f32[5,8,8,128]{3,2,1,0:T(8,128)} %param.15) | copy-start | bytes 491524
  2.4 16.2 %copy-start.54 = (f32[64,4]{0,1:T(4,128)S(1)}, f32[64,4]{0,1:T(4,128)}, u32[]{:S(2)}) copy-start(f32[64,4]{0,1:T(4,128)} %param.19) | copy-start | bytes 3076
  2.4 9.8 %collective-permute-start.1 = (f32[6,4,8,128]{3,2,1,0:T(8,128)S(1)}, f32[6,4,8,128]{3,2,1,0:T(8,128)S(1)}, u32[]{:S(2)}, u32[]{:S(2)}) collective-permute-start(f32[6,4,8,128]{3,2,1,0:T(8,128)S(1)} %get-tuple-element.203), channel_id=1, source_target_pairs={{8,0},{16,8},{24,16},{32,24},{40,32},{48,40},{56,48},{64,56},{72,6... | collective-permute-start | bytes 294920 | tf_op jit(solution)/shard_map/ppermute | solution.py:22
  3.7 8.5 %collective-permute-start = (f32[6,4,8,128]{3,2,1,0:T(8,128)S(1)}, f32[6,4,8,128]{3,2,1,0:T(8,128)S(1)}, u32[]{:S(2)}, u32[]{:S(2)}) collective-permute-start(f32[6,4,8,128]{3,2,1,0:T(8,128)S(1)} %get-tuple-element.202), channel_id=1, source_target_pairs={{0,8},{8,16},{16,24},{24,32},{32,40},{40,48},{48,56},{56,64},{64,7... | collective-permute-start | bytes 294920 | tf_op jit(solution)/shard_map/ppermute | solution.py:20
  12.4 9.4 %collective-permute-start.3 = (f32[6,16,4,128]{3,1,2,0:T(8,128)S(1)}, f32[6,16,4,128]{3,1,2,0:T(8,128)S(1)}, u32[]{:S(2)}, u32[]{:S(2)}) collective-permute-start(f32[6,16,4,128]{3,1,2,0:T(8,128)S(1)} %copy.254), channel_id=1, source_target_pairs={{1,0},{2,1},{3,2},{4,3},{5,4},{6,5},{7,6},{9,8},{10,9},{11,10},{12... | collective-permute-start | bytes 589832 | tf_op jit(solution)/shard_map/ppermute | solution.py:22
  16.6 11.7 %collective-permute-start.2 = (f32[6,16,4,128]{3,1,2,0:T(8,128)S(1)}, f32[6,16,4,128]{3,1,2,0:T(8,128)S(1)}, u32[]{:S(2)}, u32[]{:S(2)}) collective-permute-start(f32[6,16,4,128]{3,1,2,0:T(8,128)S(1)} %copy.253), channel_id=1, source_target_pairs={{0,1},{1,2},{2,3},{3,4},{4,5},{5,6},{6,7},{8,9},{9,10},{10,11},{11... | collective-permute-start | bytes 589832 | tf_op jit(solution)/shard_map/ppermute | solution.py:20
  45.3 5.1 %copy-start.22 = (f32[10,10,128]{2,1,0:T(8,128)}, f32[10,10,128]{2,1,0:T(8,128)S(1)}, u32[]{:S(2)}) copy-start(f32[10,10,128]{2,1,0:T(8,128)S(1)} %convert_multiply_fusion.3) | copy-start | bytes 153604
  46.0 35.0 %copy-start.15 = (f32[10,10,128]{2,1,0:T(8,128)}, f32[10,10,128]{2,1,0:T(8,128)S(1)}, u32[]{:S(2)}) copy-start(f32[10,10,128]{2,1,0:T(8,128)S(1)} %subtract_multiply_fusion.14) | copy-start | bytes 153604
  46.1 20.0 %copy-start.17 = (f32[10,10,128]{2,1,0:T(8,128)}, f32[10,10,128]{2,1,0:T(8,128)S(1)}, u32[]{:S(2)}) copy-start(f32[10,10,128]{2,1,0:T(8,128)S(1)} %subtract_multiply_fusion.15) | copy-start | bytes 153604
  46.2 19.3 %copy-start.19 = (f32[10,10,128]{2,1,0:T(8,128)}, f32[10,10,128]{2,1,0:T(8,128)S(1)}, u32[]{:S(2)}) copy-start(f32[10,10,128]{2,1,0:T(8,128)S(1)} %subtract_multiply_fusion.16) | copy-start | bytes 153604
  50.4 2.2 %copy-start.53 = (f32[5,256]{1,0:T(8,128)S(1)}, f32[5,256]{1,0:T(8,128)}, u32[]{:S(2)}) copy-start(f32[5,256]{1,0:T(8,128)} %param.18) | copy-start | bytes 15364
  54.3 14.8 %collective-permute-start.4 = (f32[5,8,1,128]{3,1,2,0:T(8,128)S(1)}, f32[5,8,1,128]{3,1,2,0:T(8,128)S(1)}, u32[]{:S(2)}, u32[]{:S(2)}) collective-permute-start(f32[5,8,1,128]{3,1,2,0:T(8,128)S(1)} %bitcast.155), channel_id=1, source_target_pairs={{0,1},{1,2},{2,3},{3,4},{4,5},{5,6},{6,7},{8,9},{9,10},{10,11},{11... | collective-permute-start | bytes 61448 | tf_op jit(solution)/shard_map/ppermute | solution.py:36
  56.2 12.7 %collective-permute-start.5 = (f32[5,8,1,128]{3,1,2,0:T(8,128)S(1)}, f32[5,8,1,128]{3,1,2,0:T(8,128)S(1)}, u32[]{:S(2)}, u32[]{:S(2)}) collective-permute-start(f32[5,8,1,128]{3,1,2,0:T(8,128)S(1)} %bitcast.156), channel_id=1, source_target_pairs={{1,0},{2,1},{3,2},{4,3},{5,4},{6,5},{7,6},{9,8},{10,9},{11,10},{12... | collective-permute-start | bytes 61448 | tf_op jit(solution)/shard_map/ppermute | solution.py:37
  62.2 6.8 %collective-permute-start.7 = (f32[5,1,8,128]{3,2,1,0:T(8,128)S(1)}, f32[5,1,8,128]{3,2,1,0:T(8,128)S(1)}, u32[]{:S(2)}, u32[]{:S(2)}) collective-permute-start(f32[5,1,8,128]{3,2,1,0:T(8,128)S(1)} %get-tuple-element.220), channel_id=1, source_target_pairs={{0,8},{8,16},{16,24},{24,32},{32,40},{40,48},{48,56},{56,64},{64,7... | collective-permute-start | bytes 61448 | tf_op jit(solution)/shard_map/ppermute | solution.py:36
  63.6 5.4 %collective-permute-start.6 = (f32[5,1,8,128]{3,2,1,0:T(8,128)S(1)}, f32[5,1,8,128]{3,2,1,0:T(8,128)S(1)}, u32[]{:S(2)}, u32[]{:S(2)}) collective-permute-start(f32[5,1,8,128]{3,2,1,0:T(8,128)S(1)} %get-tuple-element.219), channel_id=1, source_target_pairs={{8,0},{16,8},{24,16},{32,24},{40,32},{48,40},{56,48},{64,56},{72,6... | collective-permute-start | bytes 61448 | tf_op jit(solution)/shard_map/ppermute | solution.py:37
  65.0 4.2 %copy-start.51 = (f32[8,8,128]{2,1,0:T(8,128)}, f32[8,8,128]{2,1,0:T(8,128)S(1)}, u32[]{:S(2)}) copy-start(f32[8,8,128]{2,1,0:T(8,128)S(1)} %convert_multiply_fusion.4) | copy-start | bytes 98308
  67.0 2.2 %copy-start.45 = (f32[8,8,128]{2,1,0:T(8,128)}, f32[8,8,128]{2,1,0:T(8,128)S(1)}, u32[]{:S(2)}) copy-start(f32[8,8,128]{2,1,0:T(8,128)S(1)} %subtract_multiply_fusion.25) | copy-start | bytes 98308
  67.1 2.2 %copy-start.47 = (f32[8,8,128]{2,1,0:T(8,128)}, f32[8,8,128]{2,1,0:T(8,128)S(1)}, u32[]{:S(2)}) copy-start(f32[8,8,128]{2,1,0:T(8,128)S(1)} %subtract_multiply_fusion.26) | copy-start | bytes 98308
  68.9 5.0 %copy-start.49 = (f32[8,8,128]{2,1,0:T(8,128)}, f32[8,8,128]{2,1,0:T(8,128)S(1)}, u32[]{:S(2)}) copy-start(f32[8,8,128]{2,1,0:T(8,128)S(1)} %subtract_multiply_fusion.27) | copy-start | bytes 98308
  74.3 7.3 %collective-permute-start.9 = (f32[5,2,8,128]{3,2,1,0:T(8,128)S(1)}, f32[5,2,8,128]{3,2,1,0:T(8,128)S(1)}, u32[]{:S(2)}, u32[]{:S(2)}) collective-permute-start(f32[5,2,8,128]{3,2,1,0:T(8,128)S(1)} %get-tuple-element.216), channel_id=1, source_target_pairs={{8,0},{16,8},{24,16},{32,24},{40,32},{48,40},{56,48},{64,56},{72,6... | collective-permute-start | bytes 122888 | tf_op jit(solution)/shard_map/ppermute | solution.py:22
  75.6 6.2 %collective-permute-start.8 = (f32[5,2,8,128]{3,2,1,0:T(8,128)S(1)}, f32[5,2,8,128]{3,2,1,0:T(8,128)S(1)}, u32[]{:S(2)}, u32[]{:S(2)}) collective-permute-start(f32[5,2,8,128]{3,2,1,0:T(8,128)S(1)} %get-tuple-element.215), channel_id=1, source_target_pairs={{0,8},{8,16},{16,24},{24,32},{32,40},{40,48},{48,56},{56,64},{64,7... | collective-permute-start | bytes 122888 | tf_op jit(solution)/shard_map/ppermute | solution.py:20
  83.2 7.3 %collective-permute-start.11 = (f32[5,12,2,128]{3,2,1,0:T(2,128)}, f32[5,12,2,128]{3,2,1,0:T(2,128)}, u32[]{:S(2)}, u32[]{:S(2)}) collective-permute-start(f32[5,12,2,128]{3,2,1,0:T(2,128)} %get-tuple-element.189), channel_id=1, source_target_pairs={{1,0},{2,1},{3,2},{4,3},{5,4},{6,5},{7,6},{9,8},{10,9},{11,10},{12... | collective-permute-start | bytes 184328 | tf_op jit(solution)/shard_map/ppermute | solution.py:22
  85.1 8.5 %collective-permute-start.10 = (f32[5,12,2,128]{3,2,1,0:T(2,128)}, f32[5,12,2,128]{3,2,1,0:T(2,128)}, u32[]{:S(2)}, u32[]{:S(2)}) collective-permute-start(f32[5,12,2,128]{3,2,1,0:T(2,128)} %get-tuple-element.188), channel_id=1, source_target_pairs={{0,1},{1,2},{2,3},{3,4},{4,5},{5,6},{6,7},{8,9},{9,10},{10,11},{11... | collective-permute-start | bytes 184328 | tf_op jit(solution)/shard_map/ppermute | solution.py:20
  95.6 1.4 copy-start.20
  95.6 1.4 copy-start.23
  95.6 1.4 copy-start.57
  97.0 3.3 %copy-start.2 = (f32[10,10,128]{2,1,0:T(8,128)S(1)}, f32[10,10,128]{2,1,0:T(8,128)}, u32[]{:S(2)}) copy-start(f32[10,10,128]{2,1,0:T(8,128)} %copy-done.1) | copy-start | bytes 153604
  97.0 3.3 %copy-start.4 = (f32[10,10,128]{2,1,0:T(8,128)S(1)}, f32[10,10,128]{2,1,0:T(8,128)}, u32[]{:S(2)}) copy-start(f32[10,10,128]{2,1,0:T(8,128)} %copy-done.3) | copy-start | bytes 153604
  97.0 3.3 %copy-start.6 = (f32[10,10,128]{2,1,0:T(8,128)S(1)}, f32[10,10,128]{2,1,0:T(8,128)}, u32[]{:S(2)}) copy-start(f32[10,10,128]{2,1,0:T(8,128)} %copy-done.5) | copy-start | bytes 153604
  97.0 3.3 %copy-start.8 = (f32[10,10,128]{2,1,0:T(8,128)S(1)}, f32[10,10,128]{2,1,0:T(8,128)}, u32[]{:S(2)}) copy-start(f32[10,10,128]{2,1,0:T(8,128)} %copy-done.7) | copy-start | bytes 153604
  100.3 1.7 copy-start.9
  100.3 1.7 copy-start.10
  102.3 4.6 %copy-start.34 = (f32[8,8,128]{2,1,0:T(8,128)S(1)}, f32[8,8,128]{2,1,0:T(8,128)}, u32[]{:S(2)}) copy-start(f32[8,8,128]{2,1,0:T(8,128)} %get-tuple-element.241) | copy-start | bytes 98308
  102.3 4.6 %copy-start.35 = (f32[8,8,128]{2,1,0:T(8,128)S(1)}, f32[8,8,128]{2,1,0:T(8,128)}, u32[]{:S(2)}) copy-start(f32[8,8,128]{2,1,0:T(8,128)} %get-tuple-element.242) | copy-start | bytes 98308
  102.3 4.6 %copy-start.36 = (f32[8,8,128]{2,1,0:T(8,128)S(1)}, f32[8,8,128]{2,1,0:T(8,128)}, u32[]{:S(2)}) copy-start(f32[8,8,128]{2,1,0:T(8,128)} %get-tuple-element.243) | copy-start | bytes 98308
  102.3 4.6 %copy-start.37 = (f32[8,8,128]{2,1,0:T(8,128)S(1)}, f32[8,8,128]{2,1,0:T(8,128)}, u32[]{:S(2)}) copy-start(f32[8,8,128]{2,1,0:T(8,128)} %get-tuple-element.244) | copy-start | bytes 98308
  102.3 4.6 %copy-start.38 = (f32[8,8,128]{2,1,0:T(8,128)S(1)}, f32[8,8,128]{2,1,0:T(8,128)}, u32[]{:S(2)}) copy-start(f32[8,8,128]{2,1,0:T(8,128)} %get-tuple-element.245) | copy-start | bytes 98308
  102.3 4.6 %copy-start.39 = (f32[8,8,128]{2,1,0:T(8,128)S(1)}, f32[8,8,128]{2,1,0:T(8,128)}, u32[]{:S(2)}) copy-start(f32[8,8,128]{2,1,0:T(8,128)} %get-tuple-element.246) | copy-start | bytes 98308
  106.7 12.1 %copy-start.24 = (f32[8,8,128]{2,1,0:T(8,128)S(1)}, f32[8,8,128]{2,1,0:T(8,128)}, u32[]{:S(2)}) copy-start(f32[8,8,128]{2,1,0:T(8,128)} %slice_bitcast_fusion.17) | copy-start | bytes 98308
  106.7 12.1 %copy-start.25 = (f32[8,8,128]{2,1,0:T(8,128)S(1)}, f32[8,8,128]{2,1,0:T(8,128)}, u32[]{:S(2)}) copy-start(f32[8,8,128]{2,1,0:T(8,128)} %slice_bitcast_fusion.16) | copy-start | bytes 98308
  106.7 12.1 %copy-start.26 = (f32[8,8,128]{2,1,0:T(8,128)S(1)}, f32[8,8,128]{2,1,0:T(8,128)}, u32[]{:S(2)}) copy-start(f32[8,8,128]{2,1,0:T(8,128)} %slice_bitcast_fusion.15) | copy-start | bytes 98308
  106.7 12.1 %copy-start.27 = (f32[8,8,128]{2,1,0:T(8,128)S(1)}, f32[8,8,128]{2,1,0:T(8,128)}, u32[]{:S(2)}) copy-start(f32[8,8,128]{2,1,0:T(8,128)} %fusion.163) | copy-start | bytes 98308
  107.3 13.0 %collective-permute-start.12 = (f32[5,8,1,128]{3,1,2,0:T(8,128)S(1)}, f32[5,8,1,128]{3,1,2,0:T(8,128)S(1)}, u32[]{:S(2)}, u32[]{:S(2)}) collective-permute-start(f32[5,8,1,128]{3,1,2,0:T(8,128)S(1)} %bitcast.158), channel_id=1, source_target_pairs={{0,1},{1,2},{2,3},{3,4},{4,5},{5,6},{6,7},{8,9},{9,10},{10,11},{11... | collective-permute-start | bytes 61448 | tf_op jit(solution)/shard_map/ppermute | solution.py:36
  109.3 11.0 %collective-permute-start.13 = (f32[5,8,1,128]{3,1,2,0:T(8,128)S(1)}, f32[5,8,1,128]{3,1,2,0:T(8,128)S(1)}, u32[]{:S(2)}, u32[]{:S(2)}) collective-permute-start(f32[5,8,1,128]{3,1,2,0:T(8,128)S(1)} %bitcast.157), channel_id=1, source_target_pairs={{1,0},{2,1},{3,2},{4,3},{5,4},{6,5},{7,6},{9,8},{10,9},{11,10},{12... | collective-permute-start | bytes 61448 | tf_op jit(solution)/shard_map/ppermute | solution.py:37
  115.3 5.2 %collective-permute-start.15 = (f32[5,1,8,128]{3,2,1,0:T(8,128)S(1)}, f32[5,1,8,128]{3,2,1,0:T(8,128)S(1)}, u32[]{:S(2)}, u32[]{:S(2)}) collective-permute-start(f32[5,1,8,128]{3,2,1,0:T(8,128)S(1)} %get-tuple-element.209), channel_id=1, source_target_pairs={{0,8},{8,16},{16,24},{24,32},{32,40},{40,48},{48,56},{56,64},{64,7... | collective-permute-start | bytes 61448 | tf_op jit(solution)/shard_map/ppermute | solution.py:36
  117.5 6.6 %collective-permute-start.14 = (f32[5,1,8,128]{3,2,1,0:T(8,128)S(1)}, f32[5,1,8,128]{3,2,1,0:T(8,128)S(1)}, u32[]{:S(2)}, u32[]{:S(2)}) collective-permute-start(f32[5,1,8,128]{3,2,1,0:T(8,128)S(1)} %get-tuple-element.208), channel_id=1, source_target_pairs={{8,0},{16,8},{24,16},{32,24},{40,32},{48,40},{56,48},{64,56},{72,6... | collective-permute-start | bytes 61448 | tf_op jit(solution)/shard_map/ppermute | solution.py:37
  118.8 1.5 copy-start.12
  119.9 4.3 %copy-start.11 = (f32[5,8,8,127]{3,2,1,0:T(8,128)S(1)}, f32[5,8,8,127]{3,2,1,0:T(8,128)}, u32[]{:S(2)}) copy-start(f32[5,8,8,127]{3,2,1,0:T(8,128)} %get-tuple-element.205) | copy-start | bytes 487684
  119.9 4.5 %copy-start.58 = (f32[64]{0:T(128)S(1)}, f32[64]{0:T(128)}, u32[]{:S(2)}) copy-start(f32[64]{0:T(128)} %param.21) | copy-start | bytes 772
  120.2 23.9 %copy-start.28 = (f32[8,8,128]{2,1,0:T(8,128)S(1)}, f32[8,8,128]{2,1,0:T(8,128)}, u32[]{:S(2)}) copy-start(f32[8,8,128]{2,1,0:T(8,128)} %get-tuple-element.117) | copy-start | bytes 98308
  120.2 23.9 %copy-start.29 = (f32[8,8,128]{2,1,0:T(8,128)S(1)}, f32[8,8,128]{2,1,0:T(8,128)}, u32[]{:S(2)}) copy-start(f32[8,8,128]{2,1,0:T(8,128)} %get-tuple-element.172) | copy-start | bytes 98308
  120.2 23.8 %copy-start.30 = (f32[8,8,128]{2,1,0:T(8,128)S(1)}, f32[8,8,128]{2,1,0:T(8,128)}, u32[]{:S(2)}) copy-start(f32[8,8,128]{2,1,0:T(8,128)} %get-tuple-element.174) | copy-start | bytes 98308
  120.2 23.8 %copy-start.31 = (f32[8,8,128]{2,1,0:T(8,128)S(1)}, f32[8,8,128]{2,1,0:T(8,128)}, u32[]{:S(2)}) copy-start(f32[8,8,128]{2,1,0:T(8,128)} %get-tuple-element.176) | copy-start | bytes 98308
  120.2 23.8 %copy-start.32 = (f32[8,8,128]{2,1,0:T(8,128)S(1)}, f32[8,8,128]{2,1,0:T(8,128)}, u32[]{:S(2)}) copy-start(f32[8,8,128]{2,1,0:T(8,128)} %get-tuple-element.119) | copy-start | bytes 98308
  120.2 23.8 %copy-start.33 = (f32[8,8,128]{2,1,0:T(8,128)S(1)}, f32[8,8,128]{2,1,0:T(8,128)}, u32[]{:S(2)}) copy-start(f32[8,8,128]{2,1,0:T(8,128)} %get-tuple-element.178) | copy-start | bytes 98308
  127.5 3.7 %collective-permute-start.16 = (f32[64,6]{0,1:T(8,128)S(1)}, f32[64,6]{0,1:T(8,128)S(1)}, u32[]{:S(2)}, u32[]{:S(2)}) collective-permute-start(f32[64,6]{0,1:T(8,128)S(1)} %add_add_fusion), channel_id=1, source_target_pairs={{0,1},{1,0},{2,3},{3,2},{4,5},{5,4},{6,7},{7,6},{8,9},{9,8},{10,11... | collective-permute-start | bytes 4616 | tf_op jit(solution)/shard_map/ppermute | solution.py:203
  131.2 5.1 %collective-permute-start.17 = (f32[64,6]{0,1:T(8,128)S(1)}, f32[64,6]{0,1:T(8,128)S(1)}, u32[]{:S(2)}, u32[]{:S(2)}) collective-permute-start(f32[64,6]{0,1:T(8,128)S(1)} %add.903), channel_id=1, source_target_pairs={{0,2},{1,3},{2,0},{3,1},{4,6},{5,7},{6,4},{7,5},{8,10},{9,11},{10,... | collective-permute-start | bytes 4616 | tf_op jit(solution)/shard_map/ppermute | solution.py:203
  136.3 3.6 %collective-permute-start.18 = (f32[64,6]{0,1:T(8,128)S(1)}, f32[64,6]{0,1:T(8,128)S(1)}, u32[]{:S(2)}, u32[]{:S(2)}) collective-permute-start(f32[64,6]{0,1:T(8,128)S(1)} %add.904), channel_id=1, source_target_pairs={{0,4},{1,5},{2,6},{3,7},{4,0},{5,1},{6,2},{7,3},{8,12},{9,13},{10,... | collective-permute-start | bytes 4616 | tf_op jit(solution)/shard_map/ppermute | solution.py:203
  139.9 1.2 collective-permute-start.19
  141.1 4.5 %collective-permute-start.20 = (f32[64,6]{0,1:T(8,128)S(1)}, f32[64,6]{0,1:T(8,128)S(1)}, u32[]{:S(2)}, u32[]{:S(2)}) collective-permute-start(f32[64,6]{0,1:T(8,128)S(1)} %add.906), channel_id=1, source_target_pairs={{0,16},{8,24},{16,0},{24,8},{32,48},{40,56},{48,32},{56,40},{64,80... | collective-permute-start | bytes 4616 | tf_op jit(solution)/shard_map/ppermute | solution.py:203
  145.6 15.1 %collective-permute-start.21 = (f32[64,6]{0,1:T(8,128)S(1)}, f32[64,6]{0,1:T(8,128)S(1)}, u32[]{:S(2)}, u32[]{:S(2)}) collective-permute-start(f32[64,6]{0,1:T(8,128)S(1)} %add.907), channel_id=1, source_target_pairs={{0,32},{8,40},{16,48},{24,56},{32,0},{40,8},{48,16},{56,24},{64,96... | collective-permute-start | bytes 4616 | tf_op jit(solution)/shard_map/ppermute | solution.py:203
  160.8 11.8 %collective-permute-start.22 = (f32[64,6]{0,1:T(8,128)S(1)}, f32[64,6]{0,1:T(8,128)S(1)}, u32[]{:S(2)}, u32[]{:S(2)}) collective-permute-start(f32[64,6]{0,1:T(8,128)S(1)} %add.908), channel_id=1, source_target_pairs={{0,64},{8,72},{16,80},{24,88},{32,96},{40,104},{48,112},{56,120},{... | collective-permute-start | bytes 4616 | tf_op jit(solution)/shard_map/ppermute | solution.py:203
  172.6 9.6 %collective-permute-start.23 = (f32[64,6]{0,1:T(8,128)S(1)}, f32[64,6]{0,1:T(8,128)S(1)}, u32[]{:S(2)}, u32[]{:S(2)}) collective-permute-start(f32[64,6]{0,1:T(8,128)S(1)} %add.909), channel_id=1, source_target_pairs={{0,128},{8,136},{16,144},{24,152},{32,160},{40,168},{48,176},{56,1... | collective-permute-start | bytes 4616 | tf_op jit(solution)/shard_map/ppermute | solution.py:203
  180.7 2.1 %copy-start.21 = (f32[5,8,8,128]{3,2,1,0:T(8,128)}, f32[5,8,8,128]{3,2,1,0:T(8,128)S(1)}, u32[]{:S(2)}) copy-start(f32[5,8,8,128]{3,2,1,0:T(8,128)S(1)} %fusion.133) | copy-start | bytes 491524
  (19 other events, 17.6 us)
